TPU v7x, 32 devices: a whole 2x2x4 slice. The times are simulated.
32 devices in a mesh: dp: 16 (over z, y, core), tensor: 2 (over x).
Axes of the slice: x: 2, y: 2, z: 4, core: 2. Of those that a mesh axis runs over, the one named last changes fastest.
Arguments:
- hidden_states: bfloat16 [8192, 2048], P('dp', 'tensor'), may hold values from -6 to 6
- norm_gain: bfloat16 [2048], replicated, may hold values from 0.25 to 1.75
- head_weight: bfloat16 [2048, 25600], P(None, ('tensor', 'dp')), may hold values from -1 to 1
- target_ids: int32 [8192], P('dp'), may hold values from 0 to 25599
- loss_mask: int32 [8192], P('dp'), may hold values from 0 to 1, as said below
- seq_lengths: int32 [16], replicated, may hold values from 1 to 4096, as said below
- slot_order: int32 [16], replicated, may hold values from 0 to 15, each once
Outputs:
- token_logprob: float32 [8192], P(('dp', 'tensor'))
- token_entropy: float32 [8192], P(('dp', 'tensor'))
- seq_mean_logprob: float32 [16], P('dp')
- seq_mean_entropy: float32 [16], P('dp')
Inputs may be any that keep to these rules, and one draw needn't show every extreme that they name: `seq_lengths`: sequences lie in packed order, one after another; their lengths sum to 8192; the longest has exactly 4096 tokens and some sequence has exactly 1 token. `slot_order`: each sequence appears once. `loss_mask`: some sequence of exactly 1 token has no scored row.
All inputs are finite; a program needn't handle non-finite values.
Results may differ from a plain program's by a relative error of at most 0.0012.
Values may be sent and summed in bfloat16 or wider, within the bound.
No kernel may reach another device: no remote copies, remote signals or barrier semaphores. Data moves between devices by JAX's collectives and lax.ppermute only.
A program may use at most 192 MiB of HBM per device.

v0:
```python
import jax
import jax.numpy as jnp
from jax import lax
from jax.sharding import PartitionSpec as P

EPS = 1e-05


def per_device(
    hidden_states, norm_gain, head_weight, target_ids, loss_mask, seq_lengths, slot_order
):
    whole = lax.all_gather(hidden_states, "tensor", axis=1, tiled=True)
    values = whole.astype(jnp.float32)
    square = jnp.mean(values * values, axis=1, keepdims=True)
    normed = (values * lax.rsqrt(square + EPS) * norm_gain.astype(jnp.float32)).astype(jnp.bfloat16)
    rows = whole.shape[0]
    groups = lax.axis_size("tensor")
    share = rows // groups
    column_base = lax.axis_index("tensor") * (head_weight.shape[1] * lax.axis_size("dp"))
    piece = lax.all_gather(head_weight, "dp", axis=1, tiled=True)
    top = jnp.full((rows,), -1e30, jnp.float32)
    total = jnp.zeros((rows,), jnp.float32)
    logits = jnp.dot(normed, piece, preferred_element_type=jnp.float32)
    columns = column_base + lax.broadcasted_iota(jnp.int32, (1, piece.shape[1]), 1)
    new_top = jnp.maximum(top, jnp.max(logits, axis=1))
    shifted = logits - new_top[:, None]
    expo = jnp.exp(shifted)
    scale = jnp.exp(top - new_top)
    new_total = jnp.sum(expo, axis=1)
    new_spread = scale * (total * (top - new_top)) + jnp.sum(expo * shifted, axis=1)
    hit = jnp.sum(jnp.where(columns == target_ids[:, None], logits, 0.0), axis=1)
    mine = lax.axis_index("tensor") * share
    row_top = lax.pmax(new_top, "tensor")
    scale = jnp.exp(new_top - row_top)
    sums = lax.psum(
        (new_total * scale, scale * (new_spread + new_total * (new_top - row_top)), hit), "tensor"
    )
    row_top = lax.dynamic_slice_in_dim(row_top, mine, share)
    row_total = lax.dynamic_slice_in_dim(sums[0], mine, share)
    row_spread = lax.dynamic_slice_in_dim(sums[1], mine, share)
    row_picked = lax.dynamic_slice_in_dim(sums[2], mine, share)
    logsum = jnp.log(row_total)
    live = lax.dynamic_slice_in_dim(loss_mask, mine, share).astype(jnp.float32)
    token_logprob = (row_picked - row_top - logsum) * live
    token_entropy = (logsum - row_spread / row_total) * live
    ends = jnp.cumsum(seq_lengths)
    position = lax.axis_index("dp") * rows + mine + jnp.arange(share, dtype=jnp.int32)
    segment = jnp.sum((position[:, None] >= ends[None, :]).astype(jnp.int32), axis=1)
    member = (segment[:, None] == slot_order[None, :]).astype(jnp.float32)
    lp_part = jnp.dot(token_logprob, member, precision=lax.Precision.HIGHEST)
    ent_part = jnp.dot(token_entropy, member, precision=lax.Precision.HIGHEST)
    count_part = jnp.dot(live, member, precision=lax.Precision.HIGHEST)
    lp_sum, ent_sum, count = lax.psum((lp_part, ent_part, count_part), ("dp", "tensor"))
    owned = lp_sum.shape[0] // lax.axis_size("dp")
    first_slot = lax.axis_index("dp") * owned
    floor = jnp.maximum(lax.dynamic_slice_in_dim(count, first_slot, owned), 1.0)
    seq_mean_logprob = lax.dynamic_slice_in_dim(lp_sum, first_slot, owned) / floor
    seq_mean_entropy = lax.dynamic_slice_in_dim(ent_sum, first_slot, owned) / floor
    return (token_logprob, token_entropy, seq_mean_logprob, seq_mean_entropy)


def solution(mesh):
    placed = (P("dp", "tensor"), P(), P(None, ("tensor", "dp")), P("dp"), P("dp"), P(), P())
    return jax.shard_map(
        per_device,
        mesh=mesh,
        in_specs=placed,
        out_specs=(P(("dp", "tensor")), P(("dp", "tensor")), P("dp"), P("dp")),
        check_vma=False,
    )
```

profile of v0, /device:TPU:0, one launch (start us, length us, event | category | flops | bytes accessed | tf_op | source)
XLA Modules:
  0.0 416.9 jit_solution(15467861116896965682)
XLA Ops:
  7.2 0.0 all-gather.3.cloned.1.call-start
  7.2 0.7 all-gather.3.cloned.1.call-update
  7.9 0.0 all-gather.5.cloned.1.call-start
  7.9 0.7 all-gather.5.cloned.1.call-update
  8.7 0.7 convert_element_type.17
  9.3 0.7 copy.13
  10.1 0.1 reduce
  10.2 0.1 convert_reduce_fusion
  10.3 35.1 %all-gather.3.cloned.1.call-done = bf16[512,2048]{1,0:T(8,128)(2,1)} async-done(((bf16[512,1024]{1,0:T(8,128)(2,1)}), bf16[512,2048]{1,0:T(8,128)(2,1)}) %all-gather.3.cloned.1.call-update) | async-done | bytes 2097168 | tf_op jit(solution)/shard_map/all_gather | solution.py:12
  45.4 2.1 fusion.1
  47.5 0.0 copy-start
  47.5 256.5 %all-gather.5.cloned.1.call-done = bf16[2048,12800]{0,1:T(8,128)(2,1)} async-done(((bf16[2048,800]{0,1:T(8,128)(2,1)}), bf16[2048,12800]{0,1:T(8,128)(2,1)}) %all-gather.5.cloned.1.call-update) | async-done | bytes 52428816 | tf_op jit(solution)/shard_map/all_gather | solution.py:20
  304.0 35.8 %fusion.17 = (f32[512]{0:T(512)S(1)}, f32[512,12800]{1,0:T(8,128)}) fusion(bf16[2048,12800]{0,1:T(8,128)(2,1)} %all-gather.5.cloned.1.call-done, bf16[512,2048]{1,0:T(8,128)(2,1)} %all-gather.3.cloned.1.call-done, f32[2048]{0:T(1024)S(1)} %convert_element_type.17, f32[512]{0:T(512)S(1)} %add_rsqrt_fusion), kind=kOutput, calls=%fused_computation.34 | convolution fusion | flops 26854293504 | bytes 80752640 | tf_op jit(solution)/shard_map/dot_general | solution.py:23
  339.9 0.0 copy-start.3
  339.9 0.0 copy-start.4
  339.9 4.9 %pmax.7 = f32[512]{0:T(512)S(1)} all-reduce(f32[512]{0:T(512)S(1)} %broadcast_maximum_fusion), channel_id=1, replica_groups=mesh['dp'=16,'tensor'=2] {'tensor'}, use_global_device_ids=true, to_apply=%region_4.5 | all-reduce | flops 512 | bytes 4096 | tf_op jit(solution)/shard_map/pmax | solution.py:33
  344.8 0.0 copy-done
  344.8 13.5 %fusion = (f32[512]{0:T(512)S(1)}, f32[512]{0:T(512)S(1)}, f32[512]{0:T(512)S(1)}) fusion(f32[512,12800]{1,0:T(8,128)} %get-tuple-element.18, f32[512]{0:T(512)S(1)} %broadcast_maximum_fusion, s32[512]{0:T(512)S(1)} %copy-done, s32[12800]{0:T(1024)S(1)} %iota_add_fusion), kind=kLoop, calls=%fused_computation.2 | loop fusion | flops 45873664 | bytes 26275840 | tf_op jit(solution)/shard_map/reduce_sum | solution.py:30
  358.3 5.0 %all-reduce.1 = (f32[512]{0:T(512)S(1)}, f32[512]{0:T(512)S(1)}, f32[512]{0:T(512)S(1)}) all-reduce(f32[512]{0:T(512)S(1)} %get-tuple-element.6, f32[512]{0:T(512)S(1)} %get-tuple-element.16, f32[512]{0:T(512)S(1)} %get-tuple-element.15), channel_id=1, replica_groups=mesh['dp'=16,'tensor'=2] {'tensor'}, use_global_device_ids=true, to_apply=%region_2.0 | all-reduce | flops 1536 | bytes 12288 | tf_op jit(solution)/shard_map/psum | solution.py:35
  363.3 0.0 copy-done.3
  363.3 0.1 subtract_multiply_fusion
  363.4 0.0 copy-start.1
  363.4 0.0 copy-done.4
  363.4 0.2 convolution_bitcast_fusion
  363.6 0.2 convolution_bitcast_fusion.1
  363.9 0.1 subtract_multiply_fusion.1
  364.0 0.0 copy-start.2
  364.0 0.2 convolution_bitcast_fusion.2
  364.2 39.7 %all-reduce = (f32[16]{0:T(128)S(1)}, f32[16]{0:T(128)S(1)}, f32[16]{0:T(128)S(1)}) all-reduce(f32[16]{0:T(128)S(1)} %convolution_bitcast_fusion.2, f32[16]{0:T(128)S(1)} %convolution_bitcast_fusion.1, f32[16]{0:T(128)S(1)} %convolution_bitcast_fusion), channel_id=1, replica_groups=mesh['dp'=16,'tensor'=2] {'dp','tensor'}, use_global_device_ids=true, to_apply=%region_11.12 | all-reduce | flops 48 | bytes 384 | tf_op jit(solution)/shard_map/psum | solution.py:53
  403.9 0.7 dynamic_slice.31
  404.6 0.6 dynamic_slice.30
  405.2 0.6 dynamic_slice.29
  407.8 0.0 copy-done.1
  407.8 0.0 copy-done.2
  (6 shorter events, 0.1 us)
Async XLA Ops:
  7.2 38.3 %all-gather.3.cloned.1.call-start = ((), (), s32[]{:S(2)}) async-start(), calls=%async_computation | async-start | bytes 3145728 | tf_op jit(solution)/shard_map/all_gather | solution.py:12
  7.9 296.1 %all-gather.5.cloned.1.call-start = ((), (), s32[]{:S(2)}) async-start(), calls=%async_computation.1 | async-start | bytes 55705600 | tf_op jit(solution)/shard_map/all_gather | solution.py:20
  47.5 297.3 %copy-start = (s32[512]{0:T(512)S(1)}, s32[512]{0:T(512)}, u32[]{:S(2)}) copy-start(s32[512]{0:T(512)} %param.10) | copy-start | bytes 6148
  339.9 23.5 %copy-start.3 = (s32[512]{0:T(512)S(1)}, s32[512]{0:T(512)}, u32[]{:S(2)}) copy-start(s32[512]{0:T(512)} %param.11) | copy-start | bytes 6148
  339.9 23.6 %copy-start.4 = (s32[16]{0:T(128)S(1)}, s32[16]{0:T(128)}, u32[]{:S(2)}) copy-start(s32[16]{0:T(128)} %param.13) | copy-start | bytes 196
  363.4 44.3 %copy-start.1 = (f32[256]{0:T(256)}, f32[256]{0:T(256)S(1)}, u32[]{:S(2)}) copy-start(f32[256]{0:T(256)S(1)} %get-tuple-element.13) | copy-start | bytes 3076
  364.0 43.8 %copy-start.2 = (f32[256]{0:T(256)}, f32[256]{0:T(256)S(1)}, u32[]{:S(2)}) copy-start(f32[256]{0:T(256)S(1)} %subtract_multiply_fusion.1) | copy-start | bytes 3076
Sparse Core Ops, SparseCore 0:
  9.5 35.8 all-gather.2
  47.0 256.9 all-gather.4
where the time goes:
time: 417 us
  waiting for transfers between devices  293 us (70%)
  blocking collectives  49.7 us (12%)
  matrix products  36.5 us (9%)
  between operations  18.3 us (4%)
  other arithmetic  16.7 us (4%)
    all_gather x1, waiting for transfers between devices, per_device(): piece = lax.all_gather(head_weight, 'dp', axis=1, tiled=True)  257 us
    psum x1, blocking collectives, per_device(): lax.psum((lp_part, ent_part, count_part), ('dp', 'tensor'))  39.7 us
    dot_general x1, matrix products, per_device(): logits = jnp.dot(normed, piece, preferred_element_type=jnp.float32)  35.8 us
    all_gather x1, waiting for transfers between devices, per_device(): whole = lax.all_gather(hidden_states, 'tensor', axis=1, tiled=True)  35.1 us
    reduce_sum x1, other arithmetic, per_device(): jnp.sum(expo * shifted, axis=1)  13.5 us
  transfers between devices with their start and end apart: 2, of which 2 were waited for; matrix products, arithmetic and copies ran while one was open for 1% of the time, Pallas kernels for 0%

commit v1 on v0

v1 whole, which is shorter than its diff:
```python
import jax
import jax.numpy as jnp
import numpy as np
from jax import lax
from jax.sharding import Mesh
from jax.sharding import PartitionSpec as P

EPS = 1e-05
ROWS = ("dh", "p", "dl")
ALL = ("dh", "p", "dl", "t")


def swap(x, name):
    return lax.ppermute(x, name, [(0, 1), (1, 0)])


def whole_rows(x, t, nt):
    if nt == 2:
        other = swap(x, "t")
        return jnp.where(t == 0, jnp.concatenate([x, other], 1), jnp.concatenate([other, x], 1))
    return lax.all_gather(x, "t", axis=1, tiled=True)


def shifted(x, s, n, dh):
    if s == 0:
        return x
    if n <= 4:
        return lax.ppermute(x, "dh", [(i, (i + s) % n) for i in range(n)])
    return None


def per_device(hidden_states, norm_gain, head_weight, target_ids, loss_mask, seq_lengths, slot_order):
    rb, dt = hidden_states.shape
    nt = lax.axis_size("t")
    n = lax.axis_size("dh")
    nd = n * 4
    d = dt * nt
    cb = head_weight.shape[1]
    t = lax.axis_index("t")
    dh = lax.axis_index("dh")
    p = lax.axis_index("p")
    dl = lax.axis_index("dl")
    b = (dh * 2 + p) * 2 + dl

    w_p = swap(head_weight, "p")
    w_pair = jnp.concatenate([head_weight, w_p], 1)
    w_all = jnp.concatenate([w_pair, swap(w_pair, "dl")], 1)
    block_of = jnp.stack([b, (dh * 2 + 1 - p) * 2 + dl, (dh * 2 + p) * 2 + 1 - dl, (dh * 2 + 1 - p) * 2 + 1 - dl])
    column = ((t * nd + block_of)[:, None] * cb + jnp.arange(cb, dtype=jnp.int32)[None, :]).reshape(-1)

    gain = norm_gain.astype(jnp.float32)
    if n > 4:
        gathered_h = lax.all_gather(hidden_states, "dh", axis=0, tiled=False)
        gathered_t = lax.all_gather(target_ids, "dh", axis=0, tiled=False)

    stats = []
    for s in range(n):
        if n > 4:
            src = (dh - s) % n
            h_s, t_s = gathered_h[src], gathered_t[src]
        else:
            h_s, t_s = shifted(hidden_states, s, n, dh), shifted(target_ids, s, n, dh)
        values = whole_rows(h_s, t, nt).astype(jnp.float32)
        square = jnp.mean(values * values, axis=1, keepdims=True)
        normed = (values * lax.rsqrt(square + EPS) * gain[None, :]).astype(jnp.bfloat16)
        logits = jnp.dot(normed, w_all, preferred_element_type=jnp.float32)
        top = jnp.max(logits, axis=1)
        shift = logits - top[:, None]
        expo = jnp.exp(shift)
        total = jnp.sum(expo, axis=1)
        spread = jnp.sum(expo * shift, axis=1)
        picked = jnp.sum(jnp.where(column[None, :] == t_s[:, None], logits, 0.0), axis=1)
        stats.append(jnp.stack([top, total, spread, picked]))
    stats = jnp.stack(stats)
    stats = jnp.take(stats, (dh - jnp.arange(n)) % n, axis=0)
    rq = rb // nt
    stats = stats.reshape(n, 4, nt, rq).transpose(0, 2, 1, 3).reshape(n * nt, 4, rq)
    got = lax.all_to_all(stats, ("dh", "t"), 0, 0, tiled=True)
    tops, totals, spreads, pickeds = got[:, 0], got[:, 1], got[:, 2], got[:, 3]
    row_top = jnp.max(tops, axis=0)
    scale = jnp.exp(tops - row_top[None, :])
    row_total = jnp.sum(totals * scale, axis=0)
    row_spread = jnp.sum(scale * (spreads + totals * (tops - row_top[None, :])), axis=0)
    row_picked = jnp.sum(pickeds, axis=0)

    logsum = jnp.log(row_total)
    live = lax.dynamic_slice_in_dim(loss_mask, t * rq, rq).astype(jnp.float32)
    token_logprob = (row_picked - row_top - logsum) * live
    token_entropy = (logsum - row_spread / row_total) * live

    seqs = slot_order.shape[0]
    ends = jnp.cumsum(seq_lengths)
    position = b * rb + t * rq + jnp.arange(rq, dtype=jnp.int32)
    segment = jnp.sum((position[:, None] >= ends[None, :]).astype(jnp.int32), axis=1)
    member = (segment[:, None] == slot_order[None, :]).astype(jnp.float32)
    lp_part = jnp.dot(token_logprob, member, precision=lax.Precision.HIGHEST)
    ent_part = jnp.dot(token_entropy, member, precision=lax.Precision.HIGHEST)
    count_part = jnp.dot(live, member, precision=lax.Precision.HIGHEST)
    k = seqs // nd
    parts = jnp.stack([lp_part, ent_part, count_part]).reshape(3, nd, k).transpose(1, 0, 2)
    parts = jnp.broadcast_to(parts[:, None], (nd, nt, 3, k)).reshape(nd * nt, 3, k)
    sums = jnp.sum(lax.all_to_all(parts, ALL, 0, 0, tiled=True), axis=0)
    floor = jnp.maximum(sums[2], 1.0)
    return (token_logprob, token_entropy, sums[0] / floor, sums[1] / floor)


def solution(mesh):
    nd, nt = mesh.devices.shape
    grid = Mesh(mesh.devices.reshape(nd // 4, 2, 2, nt), ALL)
    placed = (P(ROWS, "t"), P(), P(None, ("t",) + ROWS), P(ROWS), P(ROWS), P(), P())
    return jax.shard_map(
        per_device,
        mesh=grid,
        in_specs=placed,
        out_specs=(P(ALL), P(ALL), P(ROWS), P(ROWS)),
        check_vma=False,
    )
```

time: 417 us -> 337 us (0.81)
  waiting for transfers between devices: 293 us -> 142 us
  starting transfers between devices: 0.08 us -> 74.5 us
  blocking collectives: 49.7 us -> 9.01 us
  matrix products: 36.5 us -> 62 us
  other arithmetic: 16.7 us -> 30.7 us
  between operations: 18.3 us -> 5.14 us
  local copies, waits for them, and re-layouts: 2.58 us -> 12.8 us
    all_gather x2 -> x0, waiting for transfers between devices: 292 us -> none  [the longest x1 257 us: per_device(): piece = lax.all_gather(head_weight, 'dp', axis=1, tiled=True)]
    ppermute x0 -> x12, waiting for transfers between devices: none -> 135 us  [the longest x6 73.8 us: swap(): return lax.ppermute(x, name, [(0, 1), (1, 0)])]
    ppermute x0 -> x12, starting transfers between devices: none -> 50.9 us  [the longest x6 42.7 us: shifted(): return lax.ppermute(x, 'dh', [(i, (i + s) % n) for i in range(n)])]
    psum x2 -> x0, blocking collectives: 44.7 us -> none  [the longest x1 39.7 us: per_device(): lax.psum((lp_part, ent_part, count_part), ('dp', 'tensor'))]
    dot_general x1 -> x4, matrix products: 35.8 us -> 61.3 us  [per_device(): logits = jnp.dot(normed, w_all, preferred_element_type=jnp.float32)]
    all_to_all x0 -> x1, starting transfers between devices: none -> 23.6 us  [per_device(): got = lax.all_to_all(stats, ('dh', 't'), 0, 0, tiled=True)]
    all_to_all x0 -> x1, blocking collectives: none -> 9.01 us  [per_device(): sums = jnp.sum(lax.all_to_all(parts, ALL, 0, 0, tiled=True), axis=0)]
    reduce_sum x1 -> x4, other arithmetic: 2.07 us -> 10.5 us  [per_device(): square = jnp.mean(values * values, axis=1, keepdims=True)]
  transfers between devices with their start and end apart: 2 -> 13, of which waited for: 2 -> 5; matrix products, arithmetic and copies ran while one was open for 1% -> 25% of each run, Pallas kernels for 0% -> 0%
where the time goes in v1:
time: 337 us; the launch traced here: 336 us
  waiting for transfers between devices  142 us (42%)
  starting transfers between devices  74.5 us (22%)
  matrix products  62 us (18%)
  other arithmetic  30.7 us (9%)
  local copies, waits for them, and re-layouts  12.8 us (4%)
  blocking collectives  9.01 us (3%)
  between operations  5.14 us (2%)
    ppermute x6, waiting for transfers between devices, swap(): return lax.ppermute(x, name, [(0, 1), (1, 0)])  73.8 us
    ppermute x6, waiting for transfers between devices, shifted(): return lax.ppermute(x, 'dh', [(i, (i + s) % n) for i in range(n)])  61.7 us
    dot_general x4, matrix products, per_device(): logits = jnp.dot(normed, w_all, preferred_element_type=jnp.float32)  61.3 us
    ppermute x6, starting transfers between devices, shifted(): return lax.ppermute(x, 'dh', [(i, (i + s) % n) for i in range(n)])  42.7 us
    all_to_all x1, starting transfers between devices, per_device(): got = lax.all_to_all(stats, ('dh', 't'), 0, 0, tiled=True)  23.6 us
    reduce_sum x1, other arithmetic, per_device(): total = jnp.sum(expo, axis=1)  12.5 us
    reduce_sum x4, other arithmetic, per_device(): square = jnp.mean(values * values, axis=1, keepdims=True)  10.5 us
    all_to_all x1, blocking collectives, per_device(): sums = jnp.sum(lax.all_to_all(parts, ALL, 0, 0, tiled=True), axis=0)  9.01 us
  transfers between devices with their start and end apart: 13, of which 5 were waited for; matrix products, arithmetic and copies ran while one was open for 25% of the time, Pallas kernels for 0%

profile of v1, /device:TPU:0, one launch (start us, length us, event | category | flops | bytes accessed | tf_op | source)
XLA Modules:
  0.0 336.2 jit_solution(6759977748858192598)
XLA Ops:
  0.7 3.0 collective-permute-start.1
  3.7 71.1 %collective-permute-done.1 = bf16[2048,800]{0,1:T(8,128)(2,1)S(1)} collective-permute-done((bf16[2048,800]{0,1:T(8,128)(2,1)}, bf16[2048,800]{0,1:T(8,128)(2,1)S(1)}, u32[]{:S(2)}, u32[]{:S(2)}) %collective-permute-start.1) | collective-permute-done | bytes 3276832 | tf_op jit(solution)/shard_map/ppermute | solution.py:14
  74.8 6.9 %pad_maximum_fusion = bf16[2048,1600]{0,1:T(8,128)(2,1)} fusion(bf16[2048,800]{0,1:T(8,128)(2,1)S(1)} %collective-permute-done.1, bf16[2048,800]{0,1:T(8,128)(2,1)} %param.9), kind=kLoop, calls=%fused_computation.13 | loop fusion | flops 13107200 | bytes 13107200 | tf_op jit(solution)/shard_map/concatenate | solution.py:46
  81.7 1.9 collective-permute-start.3
  83.5 2.6 collective-permute-start.6
  86.1 1.3 collective-permute-start.9
  87.5 1.5 collective-permute-start
  89.0 0.1 fusion.50
  89.1 0.1 iota_add_fusion
  89.1 20.9 %collective-permute-done.3 = bf16[512,1024]{1,0:T(8,128)(2,1)} collective-permute-done((bf16[512,1024]{1,0:T(8,128)(2,1)}, bf16[512,1024]{1,0:T(8,128)(2,1)}, u32[]{:S(2)}, u32[]{:S(2)}) %collective-permute-start.3) | collective-permute-done | bytes 1048608 | tf_op jit(solution)/shard_map/ppermute | solution.py:28
  110.0 1.6 collective-permute-start.4
  111.7 0.1 add.147
  111.8 0.1 copy.26
  111.9 0.1 reduce.3
  112.0 1.9 constant_dynamic-update-slice_fusion.2
  114.0 40.8 %collective-permute-done.6 = bf16[512,1024]{1,0:T(8,128)(2,1)} collective-permute-done((bf16[512,1024]{1,0:T(8,128)(2,1)}, bf16[512,1024]{1,0:T(8,128)(2,1)}, u32[]{:S(2)}, u32[]{:S(2)}) %collective-permute-start.6) | collective-permute-done | bytes 1048608 | tf_op jit(solution)/shard_map/ppermute | solution.py:28
  154.7 1.5 collective-permute-start.7
  156.2 24.0 %collective-permute-start.11 = (s32[512]{0:T(512)S(1)}, s32[512]{0:T(512)S(1)}, u32[]{:S(2)}, u32[]{:S(2)}) collective-permute-start(s32[512]{0:T(512)S(1)} %copy-done.4), channel_id=1, source_target_pairs={{0,24},{8,0},{16,8},{24,16},{1,25},{9,1},{17,9},{25,17},{2,26},{10... | collective-permute-start | bytes 6152 | tf_op jit(solution)/shard_map/ppermute | solution.py:28
  180.3 0.5 collective-permute-start.10
  180.8 3.0 fusion.4
  183.9 0.1 collective-permute-start.5
  183.9 2.9 fusion.7
  186.9 12.8 %collective-permute-start.8 = (s32[512]{0:T(512)S(1)}, s32[512]{0:T(512)S(1)}, u32[]{:S(2)}, u32[]{:S(2)}) collective-permute-start(s32[512]{0:T(512)S(1)} %copy-done.4), channel_id=1, source_target_pairs={{0,16},{8,24},{16,0},{24,8},{1,17},{9,25},{17,1},{25,9},{2,18},{10... | collective-permute-start | bytes 6152 | tf_op jit(solution)/shard_map/ppermute | solution.py:28
  199.7 2.3 fusion.10
  202.0 2.7 collective-permute-done.10
  204.7 2.3 fusion.13
  207.0 1.9 constant_dynamic-update-slice_fusion.1
  208.9 6.7 %constant_dynamic-update-slice_fusion = bf16[2048,3200]{0,1:T(8,128)(2,1)} fusion(bf16[2048,3200]{0,1:T(8,128)(2,1)} %constant_dynamic-update-slice_fusion.1, bf16[2048,1600]{0,1:T(8,128)(2,1)} %collective-permute-done.2), kind=kLoop, calls=%fused_computation.83 | loop fusion | bytes 13107200 | tf_op jit(solution)/shard_map/concatenate | solution.py:47
  215.7 15.0 %fusion.58 = (f32[512]{0:T(512)S(1)}, f32[512,3200]{1,0:T(8,128)}) fusion(bf16[2048,3200]{0,1:T(8,128)(2,1)} %constant_dynamic-update-slice_fusion, f32[512]{0:T(512)S(1)} %add_rsqrt_fusion.2, f32[2048]{0:T(1024)S(1)} %convert_element_type.35, bf16[512,1024]{1,0:T(8,128)(2,1)} %collective-permute-done.3, bf16[512,1024]{1,0:T(8,128)(2,1)} %collective-permute-done.4, ...), kind=kOutput, calls=%fused_computation.118 | convolution fusion | flops 6726155776 | bytes 21770240 | tf_op jit(solution)/shard_map/dot_general | solution.py:66
  230.7 15.5 %fusion.59 = (f32[512]{0:T(512)S(1)}, f32[512,3200]{1,0:T(8,128)}) fusion(bf16[2048,3200]{0,1:T(8,128)(2,1)} %constant_dynamic-update-slice_fusion, f32[512]{0:T(512)S(1)} %add_rsqrt_fusion.1, f32[2048]{0:T(1024)S(1)} %convert_element_type.35, bf16[512,1024]{1,0:T(8,128)(2,1)} %collective-permute-done.6, bf16[512,1024]{1,0:T(8,128)(2,1)S(1)} %collective-permute-done.7, ...), kind=kOutput, calls=%fused_computation.119 | convolution fusion | flops 6726155776 | bytes 21770240 | tf_op jit(solution)/shard_map/dot_general | solution.py:66
  246.2 15.5 %fusion.60 = (f32[512]{0:T(512)S(1)}, f32[512,3200]{1,0:T(8,128)}) fusion(bf16[2048,3200]{0,1:T(8,128)(2,1)} %constant_dynamic-update-slice_fusion, f32[512]{0:T(512)S(1)} %add_rsqrt_fusion, f32[2048]{0:T(1024)S(1)} %convert_element_type.35, bf16[512,1024]{1,0:T(8,128)(2,1)} %collective-permute-done.9, bf16[512,1024]{1,0:T(8,128)(2,1)S(1)} %collective-permute-done.10, ...), kind=kOutput, calls=%fused_computation.120 | convolution fusion | flops 6726155776 | bytes 21770240 | tf_op jit(solution)/shard_map/dot_general | solution.py:66
  261.7 15.3 %fusion.57 = (f32[512]{0:T(512)S(1)}, f32[512,3200]{1,0:T(8,128)}) fusion(bf16[2048,3200]{0,1:T(8,128)(2,1)} %constant_dynamic-update-slice_fusion, f32[2048]{0:T(1024)S(1)} %convert_element_type.35, f32[512]{0:T(512)S(1)} %add_rsqrt_fusion.3, bf16[512,1024]{1,0:T(8,128)(2,1)} %param.7, bf16[512,1024]{1,0:T(8,128)(2,1)} %collective-permute-done, pred[]{:T(512)S(6)} %eq.27), kind=kOutput, calls=%fused_computation.117 | convolution fusion | flops 6726155776 | bytes 21770240 | tf_op jit(solution)/shard_map/dot_general | solution.py:66
  277.0 12.5 %exponential_reduce_fusion.3 = (f32[512]{0:T(512)S(1)}, f32[512]{0:T(512)S(1)}, f32[512]{0:T(512)S(1)}, f32[512]{0:T(512)S(1)}, f32[512]{0:T(512)S(1)}, /*index=...) fusion(f32[512,3200]{1,0:T(8,128)} %get-tuple-element.40, ...), kind=kLoop, calls=%fused_computation.8 | loop fusion | flops 45869056 | bytes 26268160 | tf_op jit(solution)/shard_map/reduce_sum | solution.py:70
  289.6 0.6 gather_fusion
  290.1 0.1 broadcast_select_fusion
  290.2 0.6 reshape.204
  290.8 23.6 %all-to-all-start = ((f32[8,4,256]{2,1,0:T(4,128)}), f32[8,4,256]{2,1,0:T(4,128)S(1)}, u32[]{:S(2)}, u32[]{:S(2)}) async-start(f32[8,4,256]{2,1,0:T(4,128)} %reshape.204), calls=%async_computation | async-start | bytes 65536 | tf_op jit(solution)/shard_map/all_to_all | solution.py:78
  314.5 0.1 convert_reduce_fusion
  314.6 6.6 %all-to-all-done = f32[8,4,256]{2,1,0:T(4,128)S(1)} async-done(((f32[8,4,256]{2,1,0:T(4,128)}), f32[8,4,256]{2,1,0:T(4,128)S(1)}, u32[]{:S(2)}, u32[]{:S(2)}) %all-to-all-start) | async-done | bytes 32800 | tf_op jit(solution)/shard_map/all_to_all | solution.py:78
  321.3 0.1 subtract_multiply_fusion
  321.3 0.0 copy-start.5
  321.4 0.2 fusion.36
  321.6 0.2 fusion.34
  321.8 0.2 fusion.32
  322.1 0.1 copy.33
  322.2 9.0 %all_to_all.10 = f32[32,3,1]{1,2,0:T(1,128)S(1)} all-to-all(f32[32,3,1]{1,2,0:T(1,128)S(1)} %bitcast.71), channel_id=1, replica_groups=mesh['dh'=4,'p'=2,'dl'=2,'t'=2] {'dh','p','dl','t'}, dimensions={0} | all-to-all | bytes 768 | tf_op jit(solution)/shard_map/all_to_all | solution.py:102
  331.2 0.1 reduce_sum.209
  331.3 0.7 fusion.56
  (48 shorter events, 0.4 us)
Async XLA Ops:
  0.6 111.4 %copy-start = (bf16[2048,800]{0,1:T(8,128)(2,1)S(1)}, bf16[2048,800]{0,1:T(8,128)(2,1)}, u32[]{:S(2)}) copy-start(bf16[2048,800]{0,1:T(8,128)(2,1)} %param.9) | copy-start | bytes 9830404
  0.6 111.1 %copy-start.3 = (bf16[2048]{0:T(1024)(128)(2,1)S(1)}, bf16[2048]{0:T(1024)(128)(2,1)}, u32[]{:S(2)}) copy-start(bf16[2048]{0:T(1024)(128)(2,1)} %param.8) | copy-start | bytes 12292
  0.7 111.1 %copy-start.7 = (s32[16]{0:T(128)S(1)}, s32[16]{0:T(128)}, u32[]{:S(2)}) copy-start(s32[16]{0:T(128)} %param.12) | copy-start | bytes 196
  0.7 74.2 %collective-permute-start.1 = (bf16[2048,800]{0,1:T(8,128)(2,1)}, bf16[2048,800]{0,1:T(8,128)(2,1)S(1)}, u32[]{:S(2)}, u32[]{:S(2)}) collective-permute-start(bf16[2048,800]{0,1:T(8,128)(2,1)} %param.9), channel_id=1, source_target_pairs={{0,4},{4,0},{1,5},{5,1},{2,6},{6,2},{3,7},{7,3},{8,12},{12,8},{9,1... | collective-permute-start | bytes 9830408 | tf_op jit(solution)/shard_map/ppermute | solution.py:14
  74.8 6.9 %copy-start.1 = (bf16[2048,800]{0,1:T(8,128)(2,1)}, bf16[2048,800]{0,1:T(8,128)(2,1)S(1)}, u32[]{:S(2)}) copy-start(bf16[2048,800]{0,1:T(8,128)(2,1)S(1)} %collective-permute-done.1) | copy-start | bytes 9830404
  81.7 74.6 %copy-start.4 = (s32[512]{0:T(512)S(1)}, s32[512]{0:T(512)}, u32[]{:S(2)}) copy-start(s32[512]{0:T(512)} %param.10) | copy-start | bytes 6148
  81.7 127.2 %collective-permute-start.2 = (bf16[2048,1600]{0,1:T(8,128)(2,1)}, bf16[2048,1600]{0,1:T(8,128)(2,1)}, u32[]{:S(2)}, u32[]{:S(2)}) collective-permute-start(bf16[2048,1600]{0,1:T(8,128)(2,1)} %pad_maximum_fusion), channel_id=1, source_target_pairs={{0,2},{2,0},{1,3},{3,1},{4,6},{6,4},{5,7},{7,5},{8,10},{10,8},{9,1... | collective-permute-start | bytes 19660808 | tf_op jit(solution)/shard_map/ppermute | solution.py:14
  81.7 28.3 %collective-permute-start.3 = (bf16[512,1024]{1,0:T(8,128)(2,1)}, bf16[512,1024]{1,0:T(8,128)(2,1)}, u32[]{:S(2)}, u32[]{:S(2)}) collective-permute-start(bf16[512,1024]{1,0:T(8,128)(2,1)} %param.7), channel_id=1, source_target_pairs={{0,8},{8,16},{16,24},{24,0},{1,9},{9,17},{17,25},{25,1},{2,10},{10... | collective-permute-start | bytes 3145736 | tf_op jit(solution)/shard_map/ppermute | solution.py:28
  83.5 71.2 %collective-permute-start.6 = (bf16[512,1024]{1,0:T(8,128)(2,1)}, bf16[512,1024]{1,0:T(8,128)(2,1)}, u32[]{:S(2)}, u32[]{:S(2)}) collective-permute-start(bf16[512,1024]{1,0:T(8,128)(2,1)} %param.7), channel_id=1, source_target_pairs={{0,16},{8,24},{16,0},{24,8},{1,17},{9,25},{17,1},{25,9},{2,18},{10... | collective-permute-start | bytes 3145736 | tf_op jit(solution)/shard_map/ppermute | solution.py:28
  86.1 70.1 %collective-permute-start.9 = (bf16[512,1024]{1,0:T(8,128)(2,1)}, bf16[512,1024]{1,0:T(8,128)(2,1)}, u32[]{:S(2)}, u32[]{:S(2)}) collective-permute-start(bf16[512,1024]{1,0:T(8,128)(2,1)} %param.7), channel_id=1, source_target_pairs={{0,24},{8,0},{16,8},{24,16},{1,25},{9,1},{17,9},{25,17},{2,26},{10... | collective-permute-start | bytes 3145736 | tf_op jit(solution)/shard_map/ppermute | solution.py:28
  87.5 92.8 %collective-permute-start = (bf16[512,1024]{1,0:T(8,128)(2,1)}, bf16[512,1024]{1,0:T(8,128)(2,1)}, u32[]{:S(2)}, u32[]{:S(2)}) collective-permute-start(bf16[512,1024]{1,0:T(8,128)(2,1)} %param.7), channel_id=1, source_target_pairs={{0,1},{1,0},{2,3},{3,2},{4,5},{5,4},{6,7},{7,6},{8,9},{9,8},{10,11... | collective-permute-start | bytes 3145736 | tf_op jit(solution)/shard_map/ppermute | solution.py:14
  110.0 73.8 %collective-permute-start.4 = (bf16[512,1024]{1,0:T(8,128)(2,1)}, bf16[512,1024]{1,0:T(8,128)(2,1)}, u32[]{:S(2)}, u32[]{:S(2)}) collective-permute-start(bf16[512,1024]{1,0:T(8,128)(2,1)} %collective-permute-done.3), channel_id=1, source_target_pairs={{0,1},{1,0},{2,3},{3,2},{4,5},{5,4},{6,7},{7,6},{8,9},{9,8},{10,11... | collective-permute-start | bytes 3145736 | tf_op jit(solution)/shard_map/ppermute | solution.py:14
  154.7 32.1 %collective-permute-start.7 = (bf16[512,1024]{1,0:T(8,128)(2,1)}, bf16[512,1024]{1,0:T(8,128)(2,1)S(1)}, u32[]{:S(2)}, u32[]{:S(2)}) collective-permute-start(bf16[512,1024]{1,0:T(8,128)(2,1)} %collective-permute-done.6), channel_id=1, source_target_pairs={{0,1},{1,0},{2,3},{3,2},{4,5},{5,4},{6,7},{7,6},{8,9},{9,8},{10,11... | collective-permute-start | bytes 3145736 | tf_op jit(solution)/shard_map/ppermute | solution.py:14
  156.2 50.7 %copy-start.2 = (bf16[2048,800]{0,1:T(8,128)(2,1)S(1)}, bf16[2048,800]{0,1:T(8,128)(2,1)}, u32[]{:S(2)}) copy-start(bf16[2048,800]{0,1:T(8,128)(2,1)} %copy-done.1) | copy-start | bytes 9830404
  156.2 120.7 %collective-permute-start.11 = (s32[512]{0:T(512)S(1)}, s32[512]{0:T(512)S(1)}, u32[]{:S(2)}, u32[]{:S(2)}) collective-permute-start(s32[512]{0:T(512)S(1)} %copy-done.4), channel_id=1, source_target_pairs={{0,24},{8,0},{16,8},{24,16},{1,25},{9,1},{17,9},{25,17},{2,26},{10... | collective-permute-start | bytes 6152 | tf_op jit(solution)/shard_map/ppermute | solution.py:28
  180.3 24.4 %collective-permute-start.10 = (bf16[512,1024]{1,0:T(8,128)(2,1)}, bf16[512,1024]{1,0:T(8,128)(2,1)S(1)}, u32[]{:S(2)}, u32[]{:S(2)}) collective-permute-start(bf16[512,1024]{1,0:T(8,128)(2,1)} %collective-permute-done.9), channel_id=1, source_target_pairs={{0,1},{1,0},{2,3},{3,2},{4,5},{5,4},{6,7},{7,6},{8,9},{9,8},{10,11... | collective-permute-start | bytes 3145736 | tf_op jit(solution)/shard_map/ppermute | solution.py:14
  183.9 93.1 %collective-permute-start.5 = (s32[512]{0:T(512)S(1)}, s32[512]{0:T(512)S(1)}, u32[]{:S(2)}, u32[]{:S(2)}) collective-permute-start(s32[512]{0:T(512)S(1)} %copy-done.4), channel_id=1, source_target_pairs={{0,8},{8,16},{16,24},{24,0},{1,9},{9,17},{17,25},{25,1},{2,10},{10... | collective-permute-start | bytes 6152 | tf_op jit(solution)/shard_map/ppermute | solution.py:28
  186.9 90.1 %collective-permute-start.8 = (s32[512]{0:T(512)S(1)}, s32[512]{0:T(512)S(1)}, u32[]{:S(2)}, u32[]{:S(2)}) collective-permute-start(s32[512]{0:T(512)S(1)} %copy-done.4), channel_id=1, source_target_pairs={{0,16},{8,24},{16,0},{24,8},{1,17},{9,25},{17,1},{25,9},{2,18},{10... | collective-permute-start | bytes 6152 | tf_op jit(solution)/shard_map/ppermute | solution.py:28
  277.0 44.3 %copy-start.8 = (s32[512]{0:T(512)S(1)}, s32[512]{0:T(512)}, u32[]{:S(2)}) copy-start(s32[512]{0:T(512)} %param.11) | copy-start | bytes 6148
  277.0 44.4 %copy-start.9 = (s32[16]{0:T(128)S(1)}, s32[16]{0:T(128)}, u32[]{:S(2)}) copy-start(s32[16]{0:T(128)} %param.13) | copy-start | bytes 196
  290.8 30.3 %all-to-all-start = ((f32[8,4,256]{2,1,0:T(4,128)}), f32[8,4,256]{2,1,0:T(4,128)S(1)}, u32[]{:S(2)}, u32[]{:S(2)}) async-start(f32[8,4,256]{2,1,0:T(4,128)} %reshape.204), calls=%async_computation | async-start | bytes 65536 | tf_op jit(solution)/shard_map/all_to_all | solution.py:78
  321.3 12.6 %copy-start.6 = (f32[256]{0:T(256)}, f32[256]{0:T(256)S(1)}, u32[]{:S(2)}) copy-start(f32[256]{0:T(256)S(1)} %get-tuple-element.20) | copy-start | bytes 3076
  321.3 12.6 %copy-start.5 = (f32[256]{0:T(256)}, f32[256]{0:T(256)S(1)}, u32[]{:S(2)}) copy-start(f32[256]{0:T(256)S(1)} %subtract_multiply_fusion.1) | copy-start | bytes 3076

commit v2 on v1

--- a/solution.py
+++ b/solution.py
@@ -14,9 +14,10 @@
     return lax.ppermute(x, name, [(0, 1), (1, 0)])
 
 
-def whole_rows(x, t, nt):
+def whole_rows(x, t, nt, other=None):
     if nt == 2:
-        other = swap(x, "t")
+        if other is None:
+            other = swap(x, "t")
         return jnp.where(t == 0, jnp.concatenate([x, other], 1), jnp.concatenate([other, x], 1))
     return lax.all_gather(x, "t", axis=1, tiled=True)
 
@@ -43,8 +44,6 @@
     b = (dh * 2 + p) * 2 + dl
 
     w_p = swap(head_weight, "p")
-    w_pair = jnp.concatenate([head_weight, w_p], 1)
-    w_all = jnp.concatenate([w_pair, swap(w_pair, "dl")], 1)
     block_of = jnp.stack([b, (dh * 2 + 1 - p) * 2 + dl, (dh * 2 + p) * 2 + 1 - dl, (dh * 2 + 1 - p) * 2 + 1 - dl])
     column = ((t * nd + block_of)[:, None] * cb + jnp.arange(cb, dtype=jnp.int32)[None, :]).reshape(-1)
 
@@ -53,14 +52,41 @@
         gathered_h = lax.all_gather(hidden_states, "dh", axis=0, tiled=False)
         gathered_t = lax.all_gather(target_ids, "dh", axis=0, tiled=False)
 
+    else:
+        extra = (2 * rb) // dt if (2 * rb) % dt == 0 else 0
+        if extra:
+            code = jnp.concatenate([target_ids // 128, target_ids % 128]).astype(jnp.bfloat16).reshape(extra, dt)
+            carried = jnp.concatenate([hidden_states, code], 0)
+            moved = [shifted(carried, s, n, dh) for s in range(1, n)]
+            moved_t = []
+        else:
+            moved = [shifted(hidden_states, s, n, dh) for s in range(1, n)]
+            moved_t = [shifted(target_ids, s, n, dh) for s in range(1, n)]
+        own_other = swap(hidden_states, "t") if nt == 2 else hidden_states
+        w_p, own_other, moved, moved_t = lax.optimization_barrier((w_p, own_other, moved, moved_t))
+        if extra:
+            moved_t = []
+            for block in moved:
+                parts = block[rb:].reshape(2, rb).astype(jnp.int32)
+                moved_t.append(parts[0] * 128 + parts[1])
+            moved = [block[:rb] for block in moved]
+
+    w_pair = jnp.concatenate([head_weight, w_p], 1)
+    w_all = jnp.concatenate([w_pair, swap(w_pair, "dl")], 1)
+
     stats = []
     for s in range(n):
         if n > 4:
             src = (dh - s) % n
             h_s, t_s = gathered_h[src], gathered_t[src]
+            values = whole_rows(h_s, t, nt)
+        elif s == 0:
+            h_s, t_s = hidden_states, target_ids
+            values = whole_rows(h_s, t, nt, own_other if nt == 2 else None)
         else:
-            h_s, t_s = shifted(hidden_states, s, n, dh), shifted(target_ids, s, n, dh)
-        values = whole_rows(h_s, t, nt).astype(jnp.float32)
+            h_s, t_s = moved[s - 1], moved_t[s - 1]
+            values = whole_rows(h_s, t, nt)
+        values = values.astype(jnp.float32)
         square = jnp.mean(values * values, axis=1, keepdims=True)
         normed = (values * lax.rsqrt(square + EPS) * gain[None, :]).astype(jnp.bfloat16)
         logits = jnp.dot(normed, w_all, preferred_element_type=jnp.float32)

time: 337 us -> 290 us (0.86)
  starting transfers between devices: 74.5 us -> 40.4 us
  waiting for transfers between devices: 142 us -> 135 us
  other arithmetic: 30.7 us -> 26.1 us
    ppermute x6 -> x3, starting transfers between devices: 42.7 us -> 5.57 us  [shifted(): return lax.ppermute(x, 'dh', [(i, (i + s) % n) for i in range(n)])]
    ppermute x6 -> x3, waiting for transfers between devices: 61.7 us -> 43.1 us  [shifted(): return lax.ppermute(x, 'dh', [(i, (i + s) % n) for i in range(n)])]
    ppermute x6, waiting for transfers between devices: 73.8 us -> 85.5 us  [swap(): return lax.ppermute(x, name, [(0, 1), (1, 0)])]
    reduce_sum x4 -> x2, other arithmetic: 10.5 us -> 3.15 us  [per_device(): square = jnp.mean(values * values, axis=1, keepdims=True)]
  transfers between devices with their start and end apart: 13 -> 10, of which waited for: 5 -> 6; matrix products, arithmetic and copies ran while one was open for 25% -> 3% of each run, Pallas kernels for 0% -> 0%
where the time goes in v2:
time: 290 us; the launch traced here: 289 us
  waiting for transfers between devices  135 us (47%)
  matrix products  60.1 us (21%)
  starting transfers between devices  40.4 us (14%)
  other arithmetic  26.1 us (9%)
  local copies, waits for them, and re-layouts  13.1 us (5%)
  blocking collectives  8.88 us (3%)
  between operations  5.33 us (2%)
    ppermute x6, waiting for transfers between devices, swap(): return lax.ppermute(x, name, [(0, 1), (1, 0)])  85.5 us
    dot_general x4, matrix products, per_device(): logits = jnp.dot(normed, w_all, preferred_element_type=jnp.float32)  59.4 us
    ppermute x3, waiting for transfers between devices, shifted(): return lax.ppermute(x, 'dh', [(i, (i + s) % n) for i in range(n)])  43.1 us
    all_to_all x1, starting transfers between devices, per_device(): got = lax.all_to_all(stats, ('dh', 't'), 0, 0, tiled=True)  26.5 us
    reduce_sum x1, other arithmetic, per_device(): total = jnp.sum(expo, axis=1)  12.5 us
    all_to_all x1, blocking collectives, per_device(): sums = jnp.sum(lax.all_to_all(parts, ALL, 0, 0, tiled=True), axis=0)  8.88 us
    ppermute x6, starting transfers between devices, swap(): return lax.ppermute(x, name, [(0, 1), (1, 0)])  8.31 us
    concatenate x1, other arithmetic, per_device(): w_pair = jnp.concatenate([head_weight, w_p], 1)  7.61 us
  transfers between devices with their start and end apart: 10, of which 6 were waited for; matrix products, arithmetic and copies ran while one was open for 3% of the time, Pallas kernels for 0%

profile of v2, /device:TPU:0, one launch (start us, length us, event | category | flops | bytes accessed | tf_op | source)
XLA Modules:
  0.0 289.1 jit_solution(3887060860307894438)
XLA Ops:
  0.6 3.0 %collective-permute-start = (bf16[2048,800]{0,1:T(8,128)(2,1)}, bf16[2048,800]{0,1:T(8,128)(2,1)S(1)}, u32[]{:S(2)}, u32[]{:S(2)}) collective-permute-start(bf16[2048,800]{0,1:T(8,128)(2,1)} %param.9), channel_id=1, source_target_pairs={{0,4},{4,0},{1,5},{5,1},{2,6},{6,2},{3,7},{7,3},{8,12},{12,8},{9,1... | collective-permute-start | bytes 9830408 | tf_op jit(solution)/shard_map/ppermute | solution.py:14
  3.7 0.7 fusion.47
  4.4 1.3 maximum_maximum_fusion
  5.7 1.6 collective-permute-start.2
  7.3 2.6 collective-permute-start.3
  9.9 1.3 collective-permute-start.4
  11.3 1.5 collective-permute-start.1
  12.8 22.5 %collective-permute-done.1 = bf16[512,1024]{1,0:T(8,128)(2,1)S(1)} collective-permute-done((bf16[512,1024]{1,0:T(8,128)(2,1)}, bf16[512,1024]{1,0:T(8,128)(2,1)S(1)}, u32[]{:S(2)}, u32[]{:S(2)}) %collective-permute-start.1) | collective-permute-done | bytes 1048608 | tf_op jit(solution)/shard_map/ppermute | solution.py:14
  35.3 43.1 %collective-permute-done.3 = bf16[513,1024]{1,0:T(8,128)(2,1)S(1)} collective-permute-done((bf16[513,1024]{1,0:T(8,128)(2,1)S(1)}, bf16[513,1024]{1,0:T(8,128)(2,1)S(1)}, u32[]{:S(2)}, u32[]{:S(2)}) %collective-permute-start.3) | collective-permute-done | bytes 1050656 | tf_op jit(solution)/shard_map/ppermute | solution.py:29
  78.4 7.6 %pad_maximum_fusion = bf16[2048,1600]{0,1:T(8,128)(2,1)} fusion(bf16[2048,800]{0,1:T(8,128)(2,1)S(1)} %collective-permute-done, bf16[2048,800]{0,1:T(8,128)(2,1)} %param.9), kind=kLoop, calls=%fused_computation.13 | loop fusion | flops 13107200 | bytes 13107200 | tf_op jit(solution)/shard_map/concatenate | solution.py:74
  86.0 0.1 collective-permute-start.5
  86.2 0.1 fusion.53
  86.3 0.1 iota_add_fusion
  86.3 0.1 add.185
  86.4 0.1 copy.26
  86.5 0.1 reduce.3
  86.8 1.9 constant_dynamic-update-slice_fusion.2
  88.7 0.1 slice.72
  88.8 1.6 collective-permute-start.6
  90.3 0.1 slice.76
  90.4 0.6 collective-permute-start.7
  91.1 0.1 slice.80
  91.1 1.6 collective-permute-start.8
  92.7 1.9 constant_dynamic-update-slice_fusion.1
  94.7 20.1 %collective-permute-done.6 = bf16[512,1024]{1,0:T(8,128)(2,1)S(1)} collective-permute-done((bf16[512,1024]{1,0:T(8,128)(2,1)S(1)}, bf16[512,1024]{1,0:T(8,128)(2,1)S(1)}, u32[]{:S(2)}, u32[]{:S(2)}) %collective-permute-start.6) | collective-permute-done | bytes 1048608 | tf_op jit(solution)/shard_map/ppermute | solution.py:14
  114.8 1.6 fusion.4
  116.4 20.8 %collective-permute-done.7 = bf16[512,1024]{1,0:T(8,128)(2,1)S(1)} collective-permute-done((bf16[512,1024]{1,0:T(8,128)(2,1)S(1)}, bf16[512,1024]{1,0:T(8,128)(2,1)S(1)}, u32[]{:S(2)}, u32[]{:S(2)}) %collective-permute-start.7) | collective-permute-done | bytes 1048608 | tf_op jit(solution)/shard_map/ppermute | solution.py:14
  137.3 22.0 %collective-permute-done.8 = bf16[512,1024]{1,0:T(8,128)(2,1)S(1)} collective-permute-done((bf16[512,1024]{1,0:T(8,128)(2,1)S(1)}, bf16[512,1024]{1,0:T(8,128)(2,1)S(1)}, u32[]{:S(2)}, u32[]{:S(2)}) %collective-permute-start.8) | collective-permute-done | bytes 1048608 | tf_op jit(solution)/shard_map/ppermute | solution.py:14
  159.3 1.5 fusion.10
  160.9 6.8 %constant_dynamic-update-slice_fusion = bf16[2048,3200]{0,1:T(8,128)(2,1)} fusion(bf16[2048,3200]{0,1:T(8,128)(2,1)} %constant_dynamic-update-slice_fusion.1, bf16[2048,1600]{0,1:T(8,128)(2,1)} %collective-permute-done.5), kind=kLoop, calls=%fused_computation.84 | loop fusion | bytes 13107200 | tf_op jit(solution)/shard_map/concatenate | solution.py:75
  167.6 15.4 %fusion.60 = (f32[512]{0:T(512)S(1)}, f32[512,3200]{1,0:T(8,128)}) fusion(bf16[2048,3200]{0,1:T(8,128)(2,1)} %constant_dynamic-update-slice_fusion, f32[2048]{0:T(1024)S(1)} %convert_element_type.55, f32[512]{0:T(512)S(1)} %add_rsqrt_fusion.3, bf16[512,1024]{1,0:T(8,128)(2,1)S(1)} %copy-done.3, bf16[512,1024]{1,0:T(8,128)(2,1)} %copy-done.6, pred[]{:T(512)S(6)} %eq.29), kind=kOutput, calls=%fused_computation.137 | convolution fusion | flops 6726155776 | bytes 21770240 | tf_op jit(solution)/shard_map/dot_general | solution.py:92
  183.0 15.4 %fusion.61 = (f32[512]{0:T(512)S(1)}, f32[512,3200]{1,0:T(8,128)}) fusion(bf16[2048,3200]{0,1:T(8,128)(2,1)} %constant_dynamic-update-slice_fusion, f32[512]{0:T(512)S(1)} %add_rsqrt_fusion.2, f32[2048]{0:T(1024)S(1)} %convert_element_type.55, bf16[512,1024]{1,0:T(8,128)(2,1)S(1)} %slice.72, bf16[512,1024]{1,0:T(8,128)(2,1)} %copy-done.8, pred[]{:T(512)S(6)} %eq.29), kind=kOutput, calls=%fused_computation.138 | convolution fusion | flops 6726155776 | bytes 21770240 | tf_op jit(solution)/shard_map/dot_general | solution.py:92
  198.4 15.6 %fusion.62 = (f32[512]{0:T(512)S(1)}, f32[512,3200]{1,0:T(8,128)}) fusion(bf16[2048,3200]{0,1:T(8,128)(2,1)} %constant_dynamic-update-slice_fusion, f32[512]{0:T(512)S(1)} %add_rsqrt_fusion.1, f32[2048]{0:T(1024)S(1)} %convert_element_type.55, bf16[512,1024]{1,0:T(8,128)(2,1)S(1)} %copy-done.5, bf16[512,1024]{1,0:T(8,128)(2,1)} %copy-done.11, pred[]{:T(512)S(6)} %eq.29), kind=kOutput, calls=%fused_computation.139 | convolution fusion | flops 6726155776 | bytes 21770240 | tf_op jit(solution)/shard_map/dot_general | solution.py:92
  214.1 13.0 %fusion.63 = (f32[512]{0:T(512)S(1)}, f32[512,3200]{1,0:T(8,128)}) fusion(bf16[2048,3200]{0,1:T(8,128)(2,1)} %constant_dynamic-update-slice_fusion, f32[512]{0:T(512)S(1)} %add_rsqrt_fusion, f32[2048]{0:T(1024)S(1)} %convert_element_type.55, bf16[512,1024]{1,0:T(8,128)(2,1)S(1)} %slice.80, bf16[512,1024]{1,0:T(8,128)(2,1)S(1)} %copy-done.10, pred[]{:T(512)S(6)} %eq.29), kind=kOutput, calls=%fused_computation.140 | convolution fusion | flops 6726155776 | bytes 21770240 | tf_op jit(solution)/shard_map/dot_general | solution.py:92
  227.1 12.5 %exponential_reduce_fusion.3 = (f32[512]{0:T(512)S(1)}, f32[512]{0:T(512)S(1)}, f32[512]{0:T(512)S(1)}, f32[512]{0:T(512)S(1)}, f32[512]{0:T(512)S(1)}, /*index=...) fusion(f32[512,3200]{1,0:T(8,128)} %get-tuple-element.52, ...), kind=kLoop, calls=%fused_computation.8 | loop fusion | flops 45869056 | bytes 26268160 | tf_op jit(solution)/shard_map/reduce_sum | solution.py:96
  239.7 0.6 gather_fusion
  240.3 0.1 broadcast_select_fusion
  240.4 0.6 reshape.287
  241.0 26.5 %all-to-all-start = ((f32[8,4,256]{2,1,0:T(4,128)}), f32[8,4,256]{2,1,0:T(4,128)S(1)}, u32[]{:S(2)}, u32[]{:S(2)}) async-start(f32[8,4,256]{2,1,0:T(4,128)} %reshape.287), calls=%async_computation | async-start | bytes 65536 | tf_op jit(solution)/shard_map/all_to_all | solution.py:104
  267.5 0.1 convert_reduce_fusion
  267.6 6.6 %all-to-all-done = f32[8,4,256]{2,1,0:T(4,128)S(1)} async-done(((f32[8,4,256]{2,1,0:T(4,128)}), f32[8,4,256]{2,1,0:T(4,128)S(1)}, u32[]{:S(2)}, u32[]{:S(2)}) %all-to-all-start) | async-done | bytes 32800 | tf_op jit(solution)/shard_map/all_to_all | solution.py:104
  274.3 0.1 subtract_multiply_fusion
  274.4 0.2 fusion.32
  274.6 0.2 fusion.34
  274.9 0.2 fusion.36
  275.1 0.1 copy.33
  275.2 8.9 %all_to_all.10 = f32[32,3,1]{1,2,0:T(1,128)S(1)} all-to-all(f32[32,3,1]{1,2,0:T(1,128)S(1)} %bitcast.74), channel_id=1, replica_groups=mesh['dh'=4,'p'=2,'dl'=2,'t'=2] {'dh','p','dl','t'}, dimensions={0} | all-to-all | bytes 768 | tf_op jit(solution)/shard_map/all_to_all | solution.py:128
  284.2 0.7 fusion.59
  (84 shorter events, 0.5 us)
Async XLA Ops:
  0.6 77.8 %collective-permute-start = (bf16[2048,800]{0,1:T(8,128)(2,1)}, bf16[2048,800]{0,1:T(8,128)(2,1)S(1)}, u32[]{:S(2)}, u32[]{:S(2)}) collective-permute-start(bf16[2048,800]{0,1:T(8,128)(2,1)} %param.9), channel_id=1, source_target_pairs={{0,4},{4,0},{1,5},{5,1},{2,6},{6,2},{3,7},{7,3},{8,12},{12,8},{9,1... | collective-permute-start | bytes 9830408 | tf_op jit(solution)/shard_map/ppermute | solution.py:14
  5.7 80.5 %copy-start.19 = (bf16[2048]{0:T(1024)(128)(2,1)S(1)}, bf16[2048]{0:T(1024)(128)(2,1)}, u32[]{:S(2)}) copy-start(bf16[2048]{0:T(1024)(128)(2,1)} %param.8) | copy-start | bytes 12292
  5.7 80.7 %copy-start.22 = (s32[16]{0:T(128)S(1)}, s32[16]{0:T(128)}, u32[]{:S(2)}) copy-start(s32[16]{0:T(128)} %param.12) | copy-start | bytes 196
  5.7 81.0 %copy-start = (bf16[2048,800]{0,1:T(8,128)(2,1)S(1)}, bf16[2048,800]{0,1:T(8,128)(2,1)}, u32[]{:S(2)}) copy-start(bf16[2048,800]{0,1:T(8,128)(2,1)} %param.9) | copy-start | bytes 9830404
  5.7 29.6 %collective-permute-start.2 = (bf16[513,1024]{1,0:T(8,128)(2,1)S(1)}, bf16[513,1024]{1,0:T(8,128)(2,1)S(1)}, u32[]{:S(2)}, u32[]{:S(2)}) collective-permute-start(bf16[513,1024]{1,0:T(8,128)(2,1)S(1)} %maximum_maximum_fusion), channel_id=1, source_target_pairs={{0,8},{8,16},{16,24},{24,0},{1,9},{9,17},{17,25},{25,1},{2,10},{10... | collective-permute-start | bytes 3151880 | tf_op jit(solution)/shard_map/ppermute | solution.py:29
  7.3 71.0 %collective-permute-start.3 = (bf16[513,1024]{1,0:T(8,128)(2,1)S(1)}, bf16[513,1024]{1,0:T(8,128)(2,1)S(1)}, u32[]{:S(2)}, u32[]{:S(2)}) collective-permute-start(bf16[513,1024]{1,0:T(8,128)(2,1)S(1)} %maximum_maximum_fusion), channel_id=1, source_target_pairs={{0,16},{8,24},{16,0},{24,8},{1,17},{9,25},{17,1},{25,9},{2,18},{10... | collective-permute-start | bytes 3151880 | tf_op jit(solution)/shard_map/ppermute | solution.py:29
  9.9 68.5 %collective-permute-start.4 = (bf16[513,1024]{1,0:T(8,128)(2,1)S(1)}, bf16[513,1024]{1,0:T(8,128)(2,1)S(1)}, u32[]{:S(2)}, u32[]{:S(2)}) collective-permute-start(bf16[513,1024]{1,0:T(8,128)(2,1)S(1)} %maximum_maximum_fusion), channel_id=1, source_target_pairs={{0,24},{8,0},{16,8},{24,16},{1,25},{9,1},{17,9},{25,17},{2,26},{10... | collective-permute-start | bytes 3151880 | tf_op jit(solution)/shard_map/ppermute | solution.py:29
  11.3 24.0 %collective-permute-start.1 = (bf16[512,1024]{1,0:T(8,128)(2,1)}, bf16[512,1024]{1,0:T(8,128)(2,1)S(1)}, u32[]{:S(2)}, u32[]{:S(2)}) collective-permute-start(bf16[512,1024]{1,0:T(8,128)(2,1)} %param.7), channel_id=1, source_target_pairs={{0,1},{1,0},{2,3},{3,2},{4,5},{5,4},{6,7},{7,6},{8,9},{9,8},{10,11... | collective-permute-start | bytes 3145736 | tf_op jit(solution)/shard_map/ppermute | solution.py:14
  35.3 50.8 %copy-start.6 = (bf16[512,1024]{1,0:T(8,128)(2,1)}, bf16[512,1024]{1,0:T(8,128)(2,1)S(1)}, u32[]{:S(2)}) copy-start(bf16[512,1024]{1,0:T(8,128)(2,1)S(1)} %collective-permute-done.1) | copy-start | bytes 3145732
  35.3 43.1 %copy-start.16 = (bf16[513,1024]{1,0:T(8,128)(2,1)}, bf16[513,1024]{1,0:T(8,128)(2,1)S(1)}, u32[]{:S(2)}) copy-start(bf16[513,1024]{1,0:T(8,128)(2,1)S(1)} %collective-permute-done.2) | copy-start | bytes 3151876
  78.4 7.7 %copy-start.12 = (bf16[513,1024]{1,0:T(8,128)(2,1)}, bf16[513,1024]{1,0:T(8,128)(2,1)S(1)}, u32[]{:S(2)}) copy-start(bf16[513,1024]{1,0:T(8,128)(2,1)S(1)} %collective-permute-done.3) | copy-start | bytes 3151876
  78.4 7.6 %copy-start.14 = (bf16[513,1024]{1,0:T(8,128)(2,1)}, bf16[513,1024]{1,0:T(8,128)(2,1)S(1)}, u32[]{:S(2)}) copy-start(bf16[513,1024]{1,0:T(8,128)(2,1)S(1)} %collective-permute-done.4) | copy-start | bytes 3151876
  78.4 7.6 %copy-start.1 = (bf16[2048,800]{0,1:T(8,128)(2,1)}, bf16[2048,800]{0,1:T(8,128)(2,1)S(1)}, u32[]{:S(2)}) copy-start(bf16[2048,800]{0,1:T(8,128)(2,1)S(1)} %collective-permute-done) | copy-start | bytes 9830404
  86.0 74.8 %collective-permute-start.5 = (bf16[2048,1600]{0,1:T(8,128)(2,1)}, bf16[2048,1600]{0,1:T(8,128)(2,1)}, u32[]{:S(2)}, u32[]{:S(2)}) collective-permute-start(bf16[2048,1600]{0,1:T(8,128)(2,1)} %pad_maximum_fusion), channel_id=1, source_target_pairs={{0,2},{2,0},{1,3},{3,1},{4,6},{6,4},{5,7},{7,5},{8,10},{10,8},{9,1... | collective-permute-start | bytes 19660808 | tf_op jit(solution)/shard_map/ppermute | solution.py:14
  86.7 2.0 copy-start.17
  86.7 3.6 %copy-start.13 = (bf16[513,1024]{1,0:T(8,128)(2,1)S(1)}, bf16[513,1024]{1,0:T(8,128)(2,1)}, u32[]{:S(2)}) copy-start(bf16[513,1024]{1,0:T(8,128)(2,1)} %copy-done.12) | copy-start | bytes 3151876
  86.8 4.3 %copy-start.15 = (bf16[513,1024]{1,0:T(8,128)(2,1)S(1)}, bf16[513,1024]{1,0:T(8,128)(2,1)}, u32[]{:S(2)}) copy-start(bf16[513,1024]{1,0:T(8,128)(2,1)} %copy-done.14) | copy-start | bytes 3151876
  88.7 4.0 %copy-start.2 = (bf16[2048,800]{0,1:T(8,128)(2,1)S(1)}, bf16[2048,800]{0,1:T(8,128)(2,1)}, u32[]{:S(2)}) copy-start(bf16[2048,800]{0,1:T(8,128)(2,1)} %copy-done.1) | copy-start | bytes 9830404
  88.8 26.0 %collective-permute-start.6 = (bf16[512,1024]{1,0:T(8,128)(2,1)S(1)}, bf16[512,1024]{1,0:T(8,128)(2,1)S(1)}, u32[]{:S(2)}, u32[]{:S(2)}) collective-permute-start(bf16[512,1024]{1,0:T(8,128)(2,1)S(1)} %slice.72), channel_id=1, source_target_pairs={{0,1},{1,0},{2,3},{3,2},{4,5},{5,4},{6,7},{7,6},{8,9},{9,8},{10,11... | collective-permute-start | bytes 3145736 | tf_op jit(solution)/shard_map/ppermute | solution.py:14
  90.4 68.9 %copy-start.4 = (bf16[512,1024]{1,0:T(8,128)(2,1)}, bf16[512,1024]{1,0:T(8,128)(2,1)S(1)}, u32[]{:S(2)}) copy-start(bf16[512,1024]{1,0:T(8,128)(2,1)S(1)} %slice.76) | copy-start | bytes 3145732
  90.4 24.4 %copy-start.3 = (bf16[512,1024]{1,0:T(8,128)(2,1)S(1)}, bf16[512,1024]{1,0:T(8,128)(2,1)}, u32[]{:S(2)}) copy-start(bf16[512,1024]{1,0:T(8,128)(2,1)} %param.7) | copy-start | bytes 3145732
  90.4 24.4 %copy-start.7 = (bf16[512,1024]{1,0:T(8,128)(2,1)S(1)}, bf16[512,1024]{1,0:T(8,128)(2,1)}, u32[]{:S(2)}) copy-start(bf16[512,1024]{1,0:T(8,128)(2,1)} %copy-done.6) | copy-start | bytes 3145732
  90.4 46.8 %collective-permute-start.7 = (bf16[512,1024]{1,0:T(8,128)(2,1)S(1)}, bf16[512,1024]{1,0:T(8,128)(2,1)S(1)}, u32[]{:S(2)}, u32[]{:S(2)}) collective-permute-start(bf16[512,1024]{1,0:T(8,128)(2,1)S(1)} %slice.76), channel_id=1, source_target_pairs={{0,1},{1,0},{2,3},{3,2},{4,5},{5,4},{6,7},{7,6},{8,9},{9,8},{10,11... | collective-permute-start | bytes 3145736 | tf_op jit(solution)/shard_map/ppermute | solution.py:14
  91.1 68.2 %collective-permute-start.8 = (bf16[512,1024]{1,0:T(8,128)(2,1)S(1)}, bf16[512,1024]{1,0:T(8,128)(2,1)S(1)}, u32[]{:S(2)}, u32[]{:S(2)}) collective-permute-start(bf16[512,1024]{1,0:T(8,128)(2,1)S(1)} %slice.80), channel_id=1, source_target_pairs={{0,1},{1,0},{2,3},{3,2},{4,5},{5,4},{6,7},{7,6},{8,9},{9,8},{10,11... | collective-permute-start | bytes 3145736 | tf_op jit(solution)/shard_map/ppermute | solution.py:14
  114.8 46.0 %copy-start.8 = (bf16[512,1024]{1,0:T(8,128)(2,1)}, bf16[512,1024]{1,0:T(8,128)(2,1)S(1)}, u32[]{:S(2)}) copy-start(bf16[512,1024]{1,0:T(8,128)(2,1)S(1)} %collective-permute-done.6) | copy-start | bytes 3145732
  137.3 23.6 %copy-start.11 = (bf16[512,1024]{1,0:T(8,128)(2,1)}, bf16[512,1024]{1,0:T(8,128)(2,1)S(1)}, u32[]{:S(2)}) copy-start(bf16[512,1024]{1,0:T(8,128)(2,1)S(1)} %collective-permute-done.7) | copy-start | bytes 3145732
  159.3 1.6 copy-start.9
  183.0 15.4 %copy-start.5 = (bf16[512,1024]{1,0:T(8,128)(2,1)S(1)}, bf16[512,1024]{1,0:T(8,128)(2,1)}, u32[]{:S(2)}) copy-start(bf16[512,1024]{1,0:T(8,128)(2,1)} %copy-done.4) | copy-start | bytes 3145732
  198.4 15.6 %copy-start.10 = (bf16[512,1024]{1,0:T(8,128)(2,1)S(1)}, bf16[512,1024]{1,0:T(8,128)(2,1)}, u32[]{:S(2)}) copy-start(bf16[512,1024]{1,0:T(8,128)(2,1)} %copy-done.9) | copy-start | bytes 3145732
  214.1 13.0 %copy-start.18 = (s32[512]{0:T(512)S(1)}, s32[512]{0:T(512)}, u32[]{:S(2)}) copy-start(s32[512]{0:T(512)} %param.10) | copy-start | bytes 6148
  227.1 47.2 %copy-start.23 = (s32[512]{0:T(512)S(1)}, s32[512]{0:T(512)}, u32[]{:S(2)}) copy-start(s32[512]{0:T(512)} %param.11) | copy-start | bytes 6148
  227.1 47.3 %copy-start.24 = (s32[16]{0:T(128)S(1)}, s32[16]{0:T(128)}, u32[]{:S(2)}) copy-start(s32[16]{0:T(128)} %param.13) | copy-start | bytes 196
  241.0 33.2 %all-to-all-start = ((f32[8,4,256]{2,1,0:T(4,128)}), f32[8,4,256]{2,1,0:T(4,128)S(1)}, u32[]{:S(2)}, u32[]{:S(2)}) async-start(f32[8,4,256]{2,1,0:T(4,128)} %reshape.287), calls=%async_computation | async-start | bytes 65536 | tf_op jit(solution)/shard_map/all_to_all | solution.py:104
  274.4 12.5 %copy-start.21 = (f32[256]{0:T(256)}, f32[256]{0:T(256)S(1)}, u32[]{:S(2)}) copy-start(f32[256]{0:T(256)S(1)} %get-tuple-element.30) | copy-start | bytes 3076
  274.4 12.5 %copy-start.20 = (f32[256]{0:T(256)}, f32[256]{0:T(256)S(1)}, u32[]{:S(2)}) copy-start(f32[256]{0:T(256)S(1)} %subtract_multiply_fusion.1) | copy-start | bytes 3076

commit v3 on v2

--- a/solution.py
+++ b/solution.py
@@ -72,20 +72,8 @@
             moved = [block[:rb] for block in moved]
 
     w_pair = jnp.concatenate([head_weight, w_p], 1)
-    w_all = jnp.concatenate([w_pair, swap(w_pair, "dl")], 1)
 
-    stats = []
-    for s in range(n):
-        if n > 4:
-            src = (dh - s) % n
-            h_s, t_s = gathered_h[src], gathered_t[src]
-            values = whole_rows(h_s, t, nt)
-        elif s == 0:
-            h_s, t_s = hidden_states, target_ids
-            values = whole_rows(h_s, t, nt, own_other if nt == 2 else None)
-        else:
-            h_s, t_s = moved[s - 1], moved_t[s - 1]
-            values = whole_rows(h_s, t, nt)
+    def block_stats(values, t_s, w_all):
         values = values.astype(jnp.float32)
         square = jnp.mean(values * values, axis=1, keepdims=True)
         normed = (values * lax.rsqrt(square + EPS) * gain[None, :]).astype(jnp.bfloat16)
@@ -96,7 +84,43 @@
         total = jnp.sum(expo, axis=1)
         spread = jnp.sum(expo * shift, axis=1)
         picked = jnp.sum(jnp.where(column[None, :] == t_s[:, None], logits, 0.0), axis=1)
-        stats.append(jnp.stack([top, total, spread, picked]))
+        return jnp.stack([top, total, spread, picked])
+
+    def joined(x, other):
+        return jnp.where(t == 0, jnp.concatenate([x, other], 1), jnp.concatenate([other, x], 1))
+
+    stats = []
+    if n <= 4 and nt == 2:
+        w_dl = swap(w_pair, "dl")
+        other = {}
+        if n > 1:
+            w_dl, other[1] = lax.optimization_barrier((w_dl, swap(moved[0], "t")))
+        w_all = jnp.concatenate([w_pair, w_dl], 1)
+        for s in range(n):
+            if s == 0:
+                values = joined(hidden_states, own_other)
+                t_s = target_ids
+            else:
+                values = joined(moved[s - 1], other[s])
+                t_s = moved_t[s - 1]
+            block = block_stats(values, t_s, w_all)
+            if s + 2 < n:
+                block, other[s + 2] = lax.optimization_barrier((block, swap(moved[s + 1], "t")))
+            stats.append(block)
+    else:
+        w_all = jnp.concatenate([w_pair, swap(w_pair, "dl")], 1)
+        for s in range(n):
+            if n > 4:
+                src = (dh - s) % n
+                h_s, t_s = gathered_h[src], gathered_t[src]
+                values = whole_rows(h_s, t, nt)
+            elif s == 0:
+                h_s, t_s = hidden_states, target_ids
+                values = whole_rows(h_s, t, nt)
+            else:
+                h_s, t_s = moved[s - 1], moved_t[s - 1]
+                values = whole_rows(h_s, t, nt)
+            stats.append(block_stats(values, t_s, w_all))
     stats = jnp.stack(stats)
     stats = jnp.take(stats, (dh - jnp.arange(n)) % n, axis=0)
     rq = rb // nt

time: 290 us -> 255 us (0.88)
  waiting for transfers between devices: 135 us -> 91.4 us
  other arithmetic: 26.1 us -> 33.8 us
    ppermute x6, waiting for transfers between devices: 85.5 us -> 41.7 us  [swap(): return lax.ppermute(x, name, [(0, 1), (1, 0)])]
    reduce_sum x3 -> x6, other arithmetic: 15.6 us -> 24.1 us  [the longest x3 17.1 us: block_stats(): total = jnp.sum(expo, axis=1)]
  transfers between devices with their start and end apart: 10 -> 10, of which waited for: 6 -> 4; matrix products, arithmetic and copies ran while one was open for 3% -> 30% of each run, Pallas kernels for 0% -> 0%
where the time goes in v3:
time: 255 us
  waiting for transfers between devices  91.4 us (36%)
  matrix products  59.9 us (23%)
  starting transfers between devices  40.3 us (16%)
  other arithmetic  33.8 us (13%)
  local copies, waits for them, and re-layouts  15.1 us (6%)
  blocking collectives  8.88 us (3%)
  between operations  5.28 us (2%)
    dot_general x4, matrix products, block_stats(): logits = jnp.dot(normed, w_all, preferred_element_type=jnp.float32)  59.2 us
    ppermute x3, waiting for transfers between devices, shifted(): return lax.ppermute(x, 'dh', [(i, (i + s) % n) for i in range(n)])  43.1 us
    ppermute x6, waiting for transfers between devices, swap(): return lax.ppermute(x, name, [(0, 1), (1, 0)])  41.7 us
    all_to_all x1, starting transfers between devices, per_device(): got = lax.all_to_all(stats, ('dh', 't'), 0, 0, tiled=True)  26.5 us
    reduce_sum x3, other arithmetic, block_stats(): total = jnp.sum(expo, axis=1)  17.1 us
    all_to_all x1, blocking collectives, per_device(): sums = jnp.sum(lax.all_to_all(parts, ALL, 0, 0, tiled=True), axis=0)  8.88 us
    ppermute x6, starting transfers between devices, swap(): return lax.ppermute(x, name, [(0, 1), (1, 0)])  8.24 us
    reduce_sum x3, other arithmetic, block_stats(): square = jnp.mean(values * values, axis=1, keepdims=True)  7 us
  transfers between devices with their start and end apart: 10, of which 4 were waited for; matrix products, arithmetic and copies ran while one was open for 30% of the time, Pallas kernels for 0%

profile of v3, /device:TPU:0, one launch (start us, length us, event | category | flops | bytes accessed | tf_op | source)
XLA Modules:
  0.0 254.7 jit_solution(12315374482440240091)
XLA Ops:
  0.6 3.0 %collective-permute-start = (bf16[2048,800]{0,1:T(8,128)(2,1)}, bf16[2048,800]{0,1:T(8,128)(2,1)S(1)}, u32[]{:S(2)}, u32[]{:S(2)}) collective-permute-start(bf16[2048,800]{0,1:T(8,128)(2,1)} %param.9), channel_id=1, source_target_pairs={{0,4},{4,0},{1,5},{5,1},{2,6},{6,2},{3,7},{7,3},{8,12},{12,8},{9,1... | collective-permute-start | bytes 9830408 | tf_op jit(solution)/shard_map/ppermute | solution.py:14
  3.7 0.7 fusion.47
  4.4 1.3 maximum_maximum_fusion
  5.7 1.6 collective-permute-start.2
  7.3 2.6 %collective-permute-start.3 = (bf16[513,1024]{1,0:T(8,128)(2,1)S(1)}, bf16[513,1024]{1,0:T(8,128)(2,1)S(1)}, u32[]{:S(2)}, u32[]{:S(2)}) collective-permute-start(bf16[513,1024]{1,0:T(8,128)(2,1)S(1)} %maximum_maximum_fusion), channel_id=1, source_target_pairs={{0,16},{8,24},{16,0},{24,8},{1,17},{9,25},{17,1},{25,9},{2,18},{10... | collective-permute-start | bytes 3151880 | tf_op jit(solution)/shard_map/ppermute | solution.py:29
  9.9 1.3 collective-permute-start.4
  11.3 1.5 collective-permute-start.1
  12.8 22.5 %collective-permute-done.1 = bf16[512,1024]{1,0:T(8,128)(2,1)S(1)} collective-permute-done((bf16[512,1024]{1,0:T(8,128)(2,1)}, bf16[512,1024]{1,0:T(8,128)(2,1)S(1)}, u32[]{:S(2)}, u32[]{:S(2)}) %collective-permute-start.1) | collective-permute-done | bytes 1048608 | tf_op jit(solution)/shard_map/ppermute | solution.py:14
  35.3 43.1 %collective-permute-done.3 = bf16[513,1024]{1,0:T(8,128)(2,1)S(1)} collective-permute-done((bf16[513,1024]{1,0:T(8,128)(2,1)S(1)}, bf16[513,1024]{1,0:T(8,128)(2,1)S(1)}, u32[]{:S(2)}, u32[]{:S(2)}) %collective-permute-start.3) | collective-permute-done | bytes 1050656 | tf_op jit(solution)/shard_map/ppermute | solution.py:29
  78.4 1.1 copy-done.12
  79.5 6.9 %pad_maximum_fusion = bf16[2048,1600]{0,1:T(8,128)(2,1)} fusion(bf16[2048,800]{0,1:T(8,128)(2,1)S(1)} %collective-permute-done, bf16[2048,800]{0,1:T(8,128)(2,1)} %param.9), kind=kLoop, calls=%fused_computation.13 | loop fusion | flops 13107200 | bytes 13107200 | tf_op jit(solution)/shard_map/concatenate | solution.py:74
  86.3 0.1 collective-permute-start.5
  86.5 0.1 fusion.53
  86.6 0.1 iota_add_fusion
  86.6 0.1 add.185
  86.7 0.1 copy.26
  86.8 0.1 reduce.3
  87.0 1.9 constant_dynamic-update-slice_fusion.2
  89.0 1.6 collective-permute-start.6
  90.6 1.1 slice.73
  91.7 0.5 collective-permute-start.7
  92.3 1.6 collective-permute-start.8
  93.9 1.9 constant_dynamic-update-slice_fusion.1
  95.9 19.2 %collective-permute-done.6 = bf16[512,1024]{1,0:T(8,128)(2,1)S(1)} collective-permute-done((bf16[512,1024]{1,0:T(8,128)(2,1)S(1)}, bf16[512,1024]{1,0:T(8,128)(2,1)S(1)}, u32[]{:S(2)}, u32[]{:S(2)}) %collective-permute-start.6) | collective-permute-done | bytes 1048608 | tf_op jit(solution)/shard_map/ppermute | solution.py:14
  115.1 1.8 fusion.4
  116.9 6.8 %constant_dynamic-update-slice_fusion = bf16[2048,3200]{0,1:T(8,128)(2,1)} fusion(bf16[2048,3200]{0,1:T(8,128)(2,1)} %constant_dynamic-update-slice_fusion.1, bf16[2048,1600]{0,1:T(8,128)(2,1)} %collective-permute-done.5), kind=kLoop, calls=%fused_computation.84 | loop fusion | bytes 13107200 | tf_op jit(solution)/shard_map/concatenate | solution.py:98
  123.7 15.4 %fusion.60 = (f32[512]{0:T(512)S(1)}, f32[512,3200]{1,0:T(8,128)}) fusion(bf16[2048,3200]{0,1:T(8,128)(2,1)} %constant_dynamic-update-slice_fusion, f32[2048]{0:T(1024)S(1)} %convert_element_type.55, f32[512]{0:T(512)S(1)} %add_rsqrt_fusion.3, bf16[512,1024]{1,0:T(8,128)(2,1)S(1)} %copy-done.3, bf16[512,1024]{1,0:T(8,128)(2,1)} %copy-done.4, pred[]{:T(512)S(6)} %eq.29), kind=kOutput, calls=%fused_computation.137 | convolution fusion | flops 6726155776 | bytes 21770240 | tf_op jit(solution)/shard_map/dot_general | solution.py:80
  139.1 4.6 %exponential_reduce_fusion.3 = (f32[512]{0:T(512)S(1)}, f32[512]{0:T(512)S(1)}, f32[512]{0:T(512)S(1)}) fusion(f32[512,3200]{1,0:T(8,128)} %get-tuple-element.58, f32[512]{0:T(512)S(1)} %get-tuple-element.57, s32[512]{0:T(512)S(1)} %copy-done.14, s32[3200]{0:T(1024)S(1)} %add.185), kind=kLoop, calls=%fused_computation.8 | loop fusion | flops 11467264 | bytes 6576640 | tf_op jit(solution)/shard_map/reduce_sum | solution.py:84
  143.7 2.9 %fusion.10 = f32[512]{0:T(512)S(1)} fusion(bf16[512,1024]{1,0:T(8,128)(2,1)} %slice.73, bf16[512,1024]{1,0:T(8,128)(2,1)} %collective-permute-done.7, pred[]{:T(512)S(6)} %eq.29), kind=kLoop, calls=%fused_computation.32 | loop fusion | flops 12582400 | bytes 2099201 | tf_op jit(solution)/shard_map/reduce_sum | solution.py:78
  146.7 15.1 %fusion.61 = (f32[512]{0:T(512)S(1)}, f32[512,3200]{1,0:T(8,128)}) fusion(bf16[2048,3200]{0,1:T(8,128)(2,1)} %constant_dynamic-update-slice_fusion, f32[512]{0:T(512)S(1)} %add_rsqrt_fusion.1, f32[2048]{0:T(1024)S(1)} %convert_element_type.55, bf16[512,1024]{1,0:T(8,128)(2,1)} %slice.73, bf16[512,1024]{1,0:T(8,128)(2,1)} %collective-permute-done.7, ...), kind=kOutput, calls=%fused_computation.138 | convolution fusion | flops 6726155776 | bytes 21770240 | tf_op jit(solution)/shard_map/dot_general | solution.py:80
  161.8 13.3 %fusion.62 = (f32[512]{0:T(512)S(1)}, f32[512,3200]{1,0:T(8,128)}) fusion(bf16[2048,3200]{0,1:T(8,128)(2,1)} %constant_dynamic-update-slice_fusion, f32[512]{0:T(512)S(1)} %add_rsqrt_fusion.2, f32[2048]{0:T(1024)S(1)} %convert_element_type.55, bf16[512,1024]{1,0:T(8,128)(2,1)S(1)} %slice.72, bf16[512,1024]{1,0:T(8,128)(2,1)S(1)} %copy-done.7, pred[]{:T(512)S(6)} %eq.29), kind=kOutput, calls=%fused_computation.139 | convolution fusion | flops 6726155776 | bytes 21770240 | tf_op jit(solution)/shard_map/dot_general | solution.py:80
  175.1 7.8 %exponential_reduce_fusion.1 = (f32[512]{0:T(512)S(1)}, f32[512]{0:T(512)S(1)}, f32[512]{0:T(512)S(1)}, f32[512]{0:T(512)S(1)}, f32[512]{0:T(512)S(1)}, /*index=5*/f32[512]{0:T(512)S(1)}) fusion(f32[512,3200]{1,0:T(8,128)} %get-tuple-element.60, f32[512]{0:T(512)S(1)} %get-tuple-element.59, s32[512]{0:T(512)S(1)} %bitcast.76, s32[3200]{0:T(1024)S(1)} %add.185, ...), kind=kLoop, calls=%fused_computation.4 | loop fusion | flops 22934528 | bytes 13140480 | tf_op jit(solution)/shard_map/reduce_sum | solution.py:84
  182.9 2.3 fusion.13
  185.2 15.4 %fusion.63 = (f32[512]{0:T(512)S(1)}, f32[512,3200]{1,0:T(8,128)}) fusion(bf16[2048,3200]{0,1:T(8,128)(2,1)} %constant_dynamic-update-slice_fusion, f32[512]{0:T(512)S(1)} %add_rsqrt_fusion, f32[2048]{0:T(1024)S(1)} %convert_element_type.55, bf16[512,1024]{1,0:T(8,128)(2,1)S(1)} %slice.77, bf16[512,1024]{1,0:T(8,128)(2,1)} %collective-permute-done.8, ...), kind=kOutput, calls=%fused_computation.140 | convolution fusion | flops 6726155776 | bytes 21770240 | tf_op jit(solution)/shard_map/dot_general | solution.py:80
  200.6 4.7 %exponential_reduce_fusion = (f32[512]{0:T(512)S(1)}, f32[512]{0:T(512)S(1)}, f32[512]{0:T(512)S(1)}) fusion(f32[512,3200]{1,0:T(8,128)} %get-tuple-element.64, f32[512]{0:T(512)S(1)} %get-tuple-element.63, s32[512]{0:T(512)S(1)} %bitcast.75, s32[3200]{0:T(1024)S(1)} %add.185), kind=kLoop, calls=%fused_computation.2 | loop fusion | flops 11467264 | bytes 6576640 | tf_op jit(solution)/shard_map/reduce_sum | solution.py:84
  205.3 0.6 gather_fusion
  205.9 0.1 broadcast_select_fusion
  206.0 0.6 reshape.287
  206.6 26.5 %all-to-all-start = ((f32[8,4,256]{2,1,0:T(4,128)}), f32[8,4,256]{2,1,0:T(4,128)S(1)}, u32[]{:S(2)}, u32[]{:S(2)}) async-start(f32[8,4,256]{2,1,0:T(4,128)} %reshape.287), calls=%async_computation | async-start | bytes 65536 | tf_op jit(solution)/shard_map/all_to_all | solution.py:128
  233.2 0.1 convert_reduce_fusion
  233.2 6.6 %all-to-all-done = f32[8,4,256]{2,1,0:T(4,128)S(1)} async-done(((f32[8,4,256]{2,1,0:T(4,128)}), f32[8,4,256]{2,1,0:T(4,128)S(1)}, u32[]{:S(2)}, u32[]{:S(2)}) %all-to-all-start) | async-done | bytes 32800 | tf_op jit(solution)/shard_map/all_to_all | solution.py:128
  239.9 0.1 subtract_multiply_fusion
  240.0 0.2 fusion.32
  240.3 0.2 fusion.34
  240.5 0.2 fusion.36
  240.8 0.1 copy.33
  240.9 8.9 %all_to_all.10 = f32[32,3,1]{1,2,0:T(1,128)S(1)} all-to-all(f32[32,3,1]{1,2,0:T(1,128)S(1)} %bitcast.72), channel_id=1, replica_groups=mesh['dh'=4,'p'=2,'dl'=2,'t'=2] {'dh','p','dl','t'}, dimensions={0} | all-to-all | bytes 768 | tf_op jit(solution)/shard_map/all_to_all | solution.py:152
  249.8 0.7 fusion.59
  (79 shorter events, 0.6 us)
Async XLA Ops:
  0.6 78.8 %collective-permute-start = (bf16[2048,800]{0,1:T(8,128)(2,1)}, bf16[2048,800]{0,1:T(8,128)(2,1)S(1)}, u32[]{:S(2)}, u32[]{:S(2)}) collective-permute-start(bf16[2048,800]{0,1:T(8,128)(2,1)} %param.9), channel_id=1, source_target_pairs={{0,4},{4,0},{1,5},{5,1},{2,6},{6,2},{3,7},{7,3},{8,12},{12,8},{9,1... | collective-permute-start | bytes 9830408 | tf_op jit(solution)/shard_map/ppermute | solution.py:14
  5.7 80.8 %copy-start.15 = (bf16[2048]{0:T(1024)(128)(2,1)S(1)}, bf16[2048]{0:T(1024)(128)(2,1)}, u32[]{:S(2)}) copy-start(bf16[2048]{0:T(1024)(128)(2,1)} %param.8) | copy-start | bytes 12292
  5.7 81.0 %copy-start.18 = (s32[16]{0:T(128)S(1)}, s32[16]{0:T(128)}, u32[]{:S(2)}) copy-start(s32[16]{0:T(128)} %param.12) | copy-start | bytes 196
  5.7 81.3 %copy-start = (bf16[2048,800]{0,1:T(8,128)(2,1)S(1)}, bf16[2048,800]{0,1:T(8,128)(2,1)}, u32[]{:S(2)}) copy-start(bf16[2048,800]{0,1:T(8,128)(2,1)} %param.9) | copy-start | bytes 9830404
  5.7 29.6 %collective-permute-start.2 = (bf16[513,1024]{1,0:T(8,128)(2,1)S(1)}, bf16[513,1024]{1,0:T(8,128)(2,1)S(1)}, u32[]{:S(2)}, u32[]{:S(2)}) collective-permute-start(bf16[513,1024]{1,0:T(8,128)(2,1)S(1)} %maximum_maximum_fusion), channel_id=1, source_target_pairs={{0,8},{8,16},{16,24},{24,0},{1,9},{9,17},{17,25},{25,1},{2,10},{10... | collective-permute-start | bytes 3151880 | tf_op jit(solution)/shard_map/ppermute | solution.py:29
  7.3 71.0 %collective-permute-start.3 = (bf16[513,1024]{1,0:T(8,128)(2,1)S(1)}, bf16[513,1024]{1,0:T(8,128)(2,1)S(1)}, u32[]{:S(2)}, u32[]{:S(2)}) collective-permute-start(bf16[513,1024]{1,0:T(8,128)(2,1)S(1)} %maximum_maximum_fusion), channel_id=1, source_target_pairs={{0,16},{8,24},{16,0},{24,8},{1,17},{9,25},{17,1},{25,9},{2,18},{10... | collective-permute-start | bytes 3151880 | tf_op jit(solution)/shard_map/ppermute | solution.py:29
  9.9 68.5 %collective-permute-start.4 = (bf16[513,1024]{1,0:T(8,128)(2,1)S(1)}, bf16[513,1024]{1,0:T(8,128)(2,1)S(1)}, u32[]{:S(2)}, u32[]{:S(2)}) collective-permute-start(bf16[513,1024]{1,0:T(8,128)(2,1)S(1)} %maximum_maximum_fusion), channel_id=1, source_target_pairs={{0,24},{8,0},{16,8},{24,16},{1,25},{9,1},{17,9},{25,17},{2,26},{10... | collective-permute-start | bytes 3151880 | tf_op jit(solution)/shard_map/ppermute | solution.py:29
  11.3 24.0 %collective-permute-start.1 = (bf16[512,1024]{1,0:T(8,128)(2,1)}, bf16[512,1024]{1,0:T(8,128)(2,1)S(1)}, u32[]{:S(2)}, u32[]{:S(2)}) collective-permute-start(bf16[512,1024]{1,0:T(8,128)(2,1)} %param.7), channel_id=1, source_target_pairs={{0,1},{1,0},{2,3},{3,2},{4,5},{5,4},{6,7},{7,6},{8,9},{9,8},{10,11... | collective-permute-start | bytes 3145736 | tf_op jit(solution)/shard_map/ppermute | solution.py:14
  35.3 51.0 %copy-start.4 = (bf16[512,1024]{1,0:T(8,128)(2,1)}, bf16[512,1024]{1,0:T(8,128)(2,1)S(1)}, u32[]{:S(2)}) copy-start(bf16[512,1024]{1,0:T(8,128)(2,1)S(1)} %collective-permute-done.1) | copy-start | bytes 3145732
  35.3 51.0 %copy-start.8 = (bf16[513,1024]{1,0:T(8,128)(2,1)}, bf16[513,1024]{1,0:T(8,128)(2,1)S(1)}, u32[]{:S(2)}) copy-start(bf16[513,1024]{1,0:T(8,128)(2,1)S(1)} %collective-permute-done.2) | copy-start | bytes 3151876
  78.4 7.9 %copy-start.10 = (bf16[513,1024]{1,0:T(8,128)(2,1)}, bf16[513,1024]{1,0:T(8,128)(2,1)S(1)}, u32[]{:S(2)}) copy-start(bf16[513,1024]{1,0:T(8,128)(2,1)S(1)} %collective-permute-done.3) | copy-start | bytes 3151876
  78.4 1.1 copy-start.12
  79.5 6.9 %copy-start.1 = (bf16[2048,800]{0,1:T(8,128)(2,1)}, bf16[2048,800]{0,1:T(8,128)(2,1)S(1)}, u32[]{:S(2)}) copy-start(bf16[2048,800]{0,1:T(8,128)(2,1)S(1)} %collective-permute-done) | copy-start | bytes 9830404
  86.3 28.7 %collective-permute-start.5 = (bf16[2048,1600]{0,1:T(8,128)(2,1)}, bf16[2048,1600]{0,1:T(8,128)(2,1)}, u32[]{:S(2)}, u32[]{:S(2)}) collective-permute-start(bf16[2048,1600]{0,1:T(8,128)(2,1)} %pad_maximum_fusion), channel_id=1, source_target_pairs={{0,2},{2,0},{1,3},{3,1},{4,6},{6,4},{5,7},{7,5},{8,10},{10,8},{9,1... | collective-permute-start | bytes 19660808 | tf_op jit(solution)/shard_map/ppermute | solution.py:14
  87.0 2.0 copy-start.9
  87.0 3.6 %copy-start.11 = (bf16[513,1024]{1,0:T(8,128)(2,1)S(1)}, bf16[513,1024]{1,0:T(8,128)(2,1)}, u32[]{:S(2)}) copy-start(bf16[513,1024]{1,0:T(8,128)(2,1)} %copy-done.10) | copy-start | bytes 3151876
  87.0 5.2 %copy-start.13 = (bf16[513,1024]{1,0:T(8,128)(2,1)S(1)}, bf16[513,1024]{1,0:T(8,128)(2,1)}, u32[]{:S(2)}) copy-start(bf16[513,1024]{1,0:T(8,128)(2,1)} %copy-done.12) | copy-start | bytes 3151876
  89.0 4.9 %copy-start.2 = (bf16[2048,800]{0,1:T(8,128)(2,1)S(1)}, bf16[2048,800]{0,1:T(8,128)(2,1)}, u32[]{:S(2)}) copy-start(bf16[2048,800]{0,1:T(8,128)(2,1)} %copy-done.1) | copy-start | bytes 9830404
  89.0 26.0 %collective-permute-start.6 = (bf16[512,1024]{1,0:T(8,128)(2,1)S(1)}, bf16[512,1024]{1,0:T(8,128)(2,1)S(1)}, u32[]{:S(2)}, u32[]{:S(2)}) collective-permute-start(bf16[512,1024]{1,0:T(8,128)(2,1)S(1)} %slice.72), channel_id=1, source_target_pairs={{0,1},{1,0},{2,3},{3,2},{4,5},{5,4},{6,7},{7,6},{8,9},{9,8},{10,11... | collective-permute-start | bytes 3145736 | tf_op jit(solution)/shard_map/ppermute | solution.py:14
  91.7 52.1 %collective-permute-start.7 = (bf16[512,1024]{1,0:T(8,128)(2,1)}, bf16[512,1024]{1,0:T(8,128)(2,1)}, u32[]{:S(2)}, u32[]{:S(2)}) collective-permute-start(bf16[512,1024]{1,0:T(8,128)(2,1)} %slice.73), channel_id=1, source_target_pairs={{0,1},{1,0},{2,3},{3,2},{4,5},{5,4},{6,7},{7,6},{8,9},{9,8},{10,11... | collective-permute-start | bytes 3145736 | tf_op jit(solution)/shard_map/ppermute | solution.py:14
  92.2 22.9 %copy-start.3 = (bf16[512,1024]{1,0:T(8,128)(2,1)S(1)}, bf16[512,1024]{1,0:T(8,128)(2,1)}, u32[]{:S(2)}) copy-start(bf16[512,1024]{1,0:T(8,128)(2,1)} %param.7) | copy-start | bytes 3145732
  92.2 22.8 %copy-start.5 = (bf16[512,1024]{1,0:T(8,128)(2,1)S(1)}, bf16[512,1024]{1,0:T(8,128)(2,1)}, u32[]{:S(2)}) copy-start(bf16[512,1024]{1,0:T(8,128)(2,1)} %copy-done.4) | copy-start | bytes 3145732
  92.3 90.6 %collective-permute-start.8 = (bf16[512,1024]{1,0:T(8,128)(2,1)S(1)}, bf16[512,1024]{1,0:T(8,128)(2,1)}, u32[]{:S(2)}, u32[]{:S(2)}) collective-permute-start(bf16[512,1024]{1,0:T(8,128)(2,1)S(1)} %slice.77), channel_id=1, source_target_pairs={{0,1},{1,0},{2,3},{3,2},{4,5},{5,4},{6,7},{7,6},{8,9},{9,8},{10,11... | collective-permute-start | bytes 3145736 | tf_op jit(solution)/shard_map/ppermute | solution.py:14
  115.1 1.8 copy-start.6
  123.7 15.4 %copy-start.14 = (s32[512]{0:T(512)S(1)}, s32[512]{0:T(512)}, u32[]{:S(2)}) copy-start(s32[512]{0:T(512)} %param.10) | copy-start | bytes 6148
  146.7 15.1 %copy-start.7 = (bf16[512,1024]{1,0:T(8,128)(2,1)S(1)}, bf16[512,1024]{1,0:T(8,128)(2,1)}, u32[]{:S(2)}) copy-start(bf16[512,1024]{1,0:T(8,128)(2,1)} %copy-done.6) | copy-start | bytes 3145732
  200.6 39.3 %copy-start.19 = (s32[512]{0:T(512)S(1)}, s32[512]{0:T(512)}, u32[]{:S(2)}) copy-start(s32[512]{0:T(512)} %param.11) | copy-start | bytes 6148
  200.6 39.4 %copy-start.20 = (s32[16]{0:T(128)S(1)}, s32[16]{0:T(128)}, u32[]{:S(2)}) copy-start(s32[16]{0:T(128)} %param.13) | copy-start | bytes 196
  206.6 33.2 %all-to-all-start = ((f32[8,4,256]{2,1,0:T(4,128)}), f32[8,4,256]{2,1,0:T(4,128)S(1)}, u32[]{:S(2)}, u32[]{:S(2)}) async-start(f32[8,4,256]{2,1,0:T(4,128)} %reshape.287), calls=%async_computation | async-start | bytes 65536 | tf_op jit(solution)/shard_map/all_to_all | solution.py:128
  240.0 12.5 %copy-start.17 = (f32[256]{0:T(256)}, f32[256]{0:T(256)S(1)}, u32[]{:S(2)}) copy-start(f32[256]{0:T(256)S(1)} %get-tuple-element.42) | copy-start | bytes 3076
  240.0 12.5 %copy-start.16 = (f32[256]{0:T(256)}, f32[256]{0:T(256)S(1)}, u32[]{:S(2)}) copy-start(f32[256]{0:T(256)S(1)} %subtract_multiply_fusion.1) | copy-start | bytes 3076
